TPU v7x, 256 devices: a whole 4x4x8 slice. The times are simulated.
256 devices in a mesh: face: 32 (over x, z), tile: 4 (over y), dp: 2 (over core).
Axes of the slice: x: 4, y: 4, z: 8, core: 2. Of those that a mesh axis runs over, the one named last changes fastest.
Arguments:
- loader: bfloat16 [2, 131072, 128], P('dp', ('face', 'tile')), may hold values from -6 to 6
- row_tile: int32 [131072], P(('face', 'tile')), may hold values from 0 to 127, as said below
- row_pixel: int32 [131072], P(('face', 'tile')), may hold values from 0 to 1023, as said below
- neighbours: int32 [128, 8], P(('face', 'tile')), may hold values from 0 to 128, as said below
- send_pixels: int32 [128, 8, 96], P(('face', 'tile')), may hold values from 0 to 1024, as said below
- halo_from: int32 [128, 420], P(('face', 'tile')), may hold values from 0 to 12288, as said below
- cotangent: bfloat16 [2, 131072, 128], P('dp', ('face', 'tile')), may hold values from -6 to 6
- kernel: bfloat16 [49, 128], replicated, may hold values from -0.875 to 0.875
- conv_bias: float32 [128], replicated, may hold values from -3 to 3
- norm_gain: float32 [128], replicated, may hold values from 0.1 to 1.9
- norm_bias: float32 [128], replicated, may hold values from -3 to 3
- weight_in: bfloat16 [128, 256], replicated, may hold values from -0.5 to 0.5
- bias_in: float32 [256], replicated, may hold values from -3 to 3
- weight_out: bfloat16 [256, 128], replicated, may hold values from -0.375 to 0.375
- bias_out: float32 [128], replicated, may hold values from -3 to 3
- layer_scale: float32 [128], replicated, may hold values from 0.3 to 1.5
Outputs:
- block_out: bfloat16 [2, 131072, 128], P('dp', ('face', 'tile'))
- field_grad: bfloat16 [2, 131072, 128], P('dp', ('face', 'tile'))
- grad_kernel: float32 [49, 128], replicated
- grad_conv_bias: float32 [128], replicated
- grad_norm_gain: float32 [128], replicated
- grad_norm_bias: float32 [128], replicated
- grad_weight_in: float32 [128, 256], replicated
- grad_bias_in: float32 [256], replicated
- grad_weight_out: float32 [256, 128], replicated
- grad_bias_out: float32 [128], replicated
- grad_layer_scale: float32 [128], replicated
Inputs may be any that keep to these rules, and one draw needn't show every extreme that they name: Tile index = row * 4 + column on a grid of 32 x 4 tiles that wraps in both directions. neighbours[u, k] is either 128 (a missing link where only three tiles meet at a corner) or the tile at offset d_k from u, d_k the k-th of (-1,-1), (-1,0), (-1,1), (0,-1), (0,1), (1,-1), (1,0), (1,1) in (row, column). send_pixels[u, k] holds the pixels of tile u read by tile neighbours[u, k], in slot order; 1024 marks an unused slot. `halo_from`: each cycle cell of tile t names a slot of a link of the sending tile whose neighbours entry is t, or holds 128 * 96 (no source); one tile reads each slot at most once. `row_tile`: the 1024 loader rows of one device hold exactly 8 rows of each tile. Over all loader rows, (row_tile, row_pixel) takes each pixel of each tile exactly once.
All inputs are finite; a program needn't handle non-finite values.
Results may differ from a plain program's by a relative error of at most 0.0067.
Values may be sent and summed in bfloat16 or wider, within the bound.
No kernel may reach another device: no remote copies, remote signals or barrier semaphores. Data moves between devices by JAX's collectives and lax.ppermute only.
A program may use at most 64 MiB of HBM per device.

v0:
```python
import math

import jax
import jax.numpy as jnp
import numpy as np
from jax import lax
from jax.sharding import PartitionSpec as P

LINK_OFFSETS = ((-1, -1), (-1, 0), (-1, 1), (0, -1), (0, 1), (1, -1), (1, 0), (1, 1))


def from_behind(value, axis, steps):
    count = lax.axis_size(axis)
    pairs = [(source, (source + steps) % count) for source in range(count)]
    return lax.ppermute(value, axis, pairs)


def tree_sum(parts, halving_axes, doubling_axes):
    flat = jnp.concatenate([part.reshape(-1) for part in parts])

    def bits_of(axes):
        steps = []
        for axis in axes:
            size = lax.axis_size(axis)
            bit = 1
            while bit < size:
                steps.append((axis, bit, size))
                bit *= 2
        return steps

    halving = bits_of(halving_axes)
    total = flat.shape[0]
    pad = (-total) % (1 << len(halving))
    buf = jnp.pad(flat, (0, pad))
    for axis, bit, size in halving:
        upper = (lax.axis_index(axis) // bit) % 2 == 1
        half = buf.shape[0] // 2
        low, high = buf[:half], buf[half:]
        keep = jnp.where(upper, high, low)
        send = jnp.where(upper, low, high)
        pairs = [(i, i ^ bit) for i in range(size)]
        buf = keep + lax.ppermute(send, axis, pairs)
    for axis, bit, size in bits_of(doubling_axes):
        buf = buf + lax.ppermute(buf, axis, [(i, i ^ bit) for i in range(size)])
    for axis, bit, size in reversed(halving):
        upper = (lax.axis_index(axis) // bit) % 2 == 1
        pairs = [(i, i ^ bit) for i in range(size)]
        got = lax.ppermute(buf, axis, pairs)
        buf = jnp.where(upper, jnp.concatenate([got, buf]), jnp.concatenate([buf, got]))
    out = []
    start = 0
    for part in parts:
        out.append(buf[start : start + part.size].reshape(part.shape))
        start += part.size
    return tuple(out)

def cycle_cells(tile_side):
    padded_side = tile_side + 6
    cell_rows, cell_cols = np.meshgrid(
        np.arange(padded_side), np.arange(padded_side), indexing="ij"
    )
    inside = (
        (cell_rows >= 3)
        & (cell_rows < tile_side + 3)
        & (cell_cols >= 3)
        & (cell_cols < tile_side + 3)
    )
    outside = (~inside).reshape(-1)
    return (cell_rows.reshape(-1)[outside], cell_cols.reshape(-1)[outside])


def depthwise(field_in, kern_in):
    return lax.conv_general_dilated(
        field_in,
        kern_in,
        (1, 1),
        "VALID",
        dimension_numbers=("NHWC", "HWIO", "NHWC"),
        feature_group_count=field_in.shape[-1],
        precision=lax.Precision.HIGHEST,
    )


def assemble(tile, cycle_data):
    side = tile.shape[0]
    wide = side + 6
    channels = tile.shape[-1]
    band = 3 * wide
    top = cycle_data[:band].reshape(3, wide, channels)
    middle = cycle_data[band : band + 6 * side].reshape(side, 6, channels)
    bottom = cycle_data[band + 6 * side :].reshape(3, wide, channels)
    centre = jnp.concatenate([middle[:, :3], tile, middle[:, 3:]], axis=1)
    return jnp.concatenate([top, centre, bottom], axis=0)


def ring_of(square, side):
    channels = square.shape[-1]
    top = square[:3].reshape(-1, channels)
    middle = jnp.concatenate([square[3 : side + 3, :3], square[3 : side + 3, side + 3 :]], axis=1)
    bottom = square[side + 3 :].reshape(-1, channels)
    return jnp.concatenate([top, middle.reshape(-1, channels), bottom], axis=0)


def shifted_conv(square, kern, out_side):
    total = None
    for di in range(7):
        for dj in range(7):
            term = square[di : di + out_side, dj : dj + out_side] * kern[di, dj]
            total = term if total is None else total + term
    return total


def tap_sums(square, d_square, side):
    return jnp.stack(
        [
            jnp.sum(square[di : di + side, dj : dj + side] * d_square, axis=(0, 1))
            for di in range(7)
            for dj in range(7)
        ]
    )


def normal_cdf(values):
    return 0.5 * (1.0 + lax.erf(values * 0.7071067811865476))


def move_links(blocks, heading):
    ups = [k for k, offset in enumerate(LINK_OFFSETS) if offset[0] == -1]
    downs = [k for k, offset in enumerate(LINK_OFFSETS) if offset[0] == 1]
    moved = list(blocks[k] for k in range(len(LINK_OFFSETS)))
    for group, step in ((ups, -heading), (downs, heading)):
        shifted = from_behind(jnp.stack([moved[k] for k in group]), "face", step)
        for place, k in enumerate(group):
            moved[k] = shifted[place]
    lefts = [k for k, offset in enumerate(LINK_OFFSETS) if offset[1] == -1]
    rights = [k for k, offset in enumerate(LINK_OFFSETS) if offset[1] == 1]
    for group, step in ((lefts, -heading), (rights, heading)):
        shifted = from_behind(jnp.stack([moved[k] for k in group]), "tile", step)
        for place, k in enumerate(group):
            moved[k] = shifted[place]
    return jnp.stack(moved)


def local(
    loader,
    row_tile,
    row_pixel,
    neighbours,
    send_pixels,
    halo_from,
    cotangent,
    kernel,
    conv_bias,
    norm_gain,
    norm_bias,
    weight_in,
    bias_in,
    weight_out,
    bias_out,
    layer_scale,
):
    grid_rows = lax.axis_size("face")
    grid_cols = lax.axis_size("tile")
    tile_count = grid_rows * grid_cols
    pixel_count = loader.shape[1]
    channels = loader.shape[2]
    capacity = send_pixels.shape[2]
    per_peer = pixel_count // tile_count
    tile_side = math.isqrt(pixel_count)
    cycle_rows, cycle_cols = cycle_cells(tile_side)
    factor = 1.0 / math.sqrt(lax.axis_size("dp") * tile_count * pixel_count)
    ordering = jnp.argsort(row_tile, stable=True)
    outgoing = loader[0][ordering].reshape(tile_count, per_peer, channels)
    labels = row_pixel[ordering].reshape(tile_count, per_peer)
    digits = jnp.concatenate([labels // 32, labels % 32], axis=1).astype(loader.dtype)
    label_row = jnp.pad(digits, ((0, 0), (0, channels - 2 * per_peer)))[:, None, :]
    parcel = lax.all_to_all(
        jnp.concatenate([outgoing, label_row], axis=1),
        ("face", "tile"),
        split_axis=0,
        concat_axis=0,
        tiled=True,
    )
    arrived = parcel[:, :per_peer]
    got = parcel[:, per_peer, : 2 * per_peer].astype(jnp.int32)
    places = got[:, :per_peer] * 32 + got[:, per_peer:]
    field = (
        jnp.zeros((pixel_count, channels), loader.dtype)
        .at[places.reshape(-1)]
        .set(arrived.reshape(-1, channels))
    )
    my_row = lax.axis_index("face")
    my_col = lax.axis_index("tile")
    row_steps = jnp.asarray([offset[0] for offset in LINK_OFFSETS], jnp.int32)
    col_steps = jnp.asarray([offset[1] for offset in LINK_OFFSETS], jnp.int32)
    sources = (my_row - row_steps) % grid_rows * grid_cols + (my_col - col_steps) % grid_cols
    senders = halo_from[0] // capacity
    matching = senders[:, None] == sources[None, :]
    link_of = jnp.sum(matching.astype(jnp.int32) * jnp.arange(8, dtype=jnp.int32)[None, :], axis=1)
    readable = jnp.any(matching, axis=1)
    recv_index = jnp.where(readable, link_of * capacity + halo_from[0] % capacity, 8 * capacity)
    live = (neighbours[0] < tile_count)[:, None, None]
    extended = jnp.concatenate([field, jnp.zeros((1, channels), field.dtype)], axis=0)
    blocks_out = jnp.where(live, extended[send_pixels[0]], jnp.zeros((), field.dtype))
    received = move_links(blocks_out, 1)
    flat_recv = jnp.concatenate(
        [received.reshape(8 * capacity, channels), jnp.zeros((1, channels), field.dtype)], axis=0
    )
    cycle_data = flat_recv[recv_index]
    padded = assemble(field.reshape(tile_side, tile_side, channels), cycle_data)
    kern_f = kernel.astype(jnp.float32).reshape(7, 7, channels)
    padded_f = padded.astype(jnp.float32)
    mixed = shifted_conv(padded_f, kern_f, tile_side).reshape(pixel_count, channels) + conv_bias
    average = jnp.mean(mixed, axis=-1, keepdims=True)
    centred = mixed - average
    inv_scale = lax.rsqrt(jnp.mean(centred * centred, axis=-1, keepdims=True) + 1e-06)
    standard = centred * inv_scale
    normed = (standard * norm_gain + norm_bias).astype(jnp.bfloat16)
    hidden = jnp.dot(normed, weight_in, preferred_element_type=jnp.float32) + bias_in
    cdf_vals = normal_cdf(hidden)
    active = (hidden * cdf_vals).astype(jnp.bfloat16)
    branch = jnp.dot(active, weight_out, preferred_element_type=jnp.float32) + bias_out
    block_out = (field.astype(jnp.float32) + layer_scale * branch).astype(jnp.bfloat16)
    grad_f = cotangent[0].astype(jnp.float32)
    g_scale = jnp.sum(grad_f * branch, axis=0) * factor
    d_branch = (grad_f * layer_scale).astype(jnp.bfloat16)
    g_w_out = jnp.dot(active.T, d_branch, preferred_element_type=jnp.float32) * factor
    g_b_out = jnp.sum(d_branch.astype(jnp.float32), axis=0) * factor
    d_active = jnp.dot(d_branch, weight_out.T, preferred_element_type=jnp.float32)
    slope = cdf_vals + hidden * jnp.exp(-0.5 * hidden * hidden) * 0.3989422804014327
    d_hidden = (d_active * slope).astype(jnp.bfloat16)
    g_w_in = jnp.dot(normed.T, d_hidden, preferred_element_type=jnp.float32) * factor
    g_b_in = jnp.sum(d_hidden.astype(jnp.float32), axis=0) * factor
    d_normed = jnp.dot(d_hidden, weight_in.T, preferred_element_type=jnp.float32)
    g_gain = jnp.sum(d_normed * standard, axis=0) * factor
    g_nbias = jnp.sum(d_normed, axis=0) * factor
    scaled = d_normed * norm_gain
    d_mixed = (
        inv_scale
        * (
            scaled
            - jnp.mean(scaled, axis=-1, keepdims=True)
            - standard * jnp.mean(scaled * standard, axis=-1, keepdims=True)
        )
    ).astype(jnp.bfloat16)
    g_cbias = jnp.sum(d_mixed.astype(jnp.float32), axis=0) * factor
    d_square = d_mixed.astype(jnp.float32).reshape(tile_side, tile_side, channels)
    d_pad = shifted_conv(
        jnp.pad(d_square, ((6, 6), (6, 6), (0, 0))), kern_f[::-1, ::-1], tile_side + 6
    )
    g_kern = tap_sums(padded_f, d_square, tile_side) * factor
    inner_grad = d_pad[3 : tile_side + 3, 3 : tile_side + 3].reshape(pixel_count, channels)
    cycle_grad = ring_of(d_pad, tile_side).astype(jnp.bfloat16)
    back_parcel = (
        jnp.zeros((8 * capacity + 1, channels), jnp.bfloat16).at[recv_index].set(cycle_grad)
    )
    back_parcel = back_parcel[: 8 * capacity].reshape(8, capacity, channels)
    returned = move_links(back_parcel, -1)
    returned = jnp.where(live, returned, jnp.zeros((), returned.dtype))
    incoming = (
        jnp.zeros((pixel_count + 1, channels), jnp.float32)
        .at[send_pixels[0].reshape(-1)]
        .add(returned.reshape(-1, channels).astype(jnp.float32))
    )
    field_grad = (grad_f + inner_grad + incoming[:pixel_count]).astype(jnp.bfloat16)
    g_kern, g_cbias, g_gain, g_nbias, g_w_in, g_b_in, g_w_out, g_b_out, g_scale = tree_sum(
        (g_kern, g_cbias, g_gain, g_nbias, g_w_in, g_b_in, g_w_out, g_b_out, g_scale),
        ("dp", "tile"),
        ("face",),
    )
    return (
        block_out[None],
        field_grad[None],
        g_kern,
        g_cbias,
        g_gain,
        g_nbias,
        g_w_in,
        g_b_in,
        g_w_out,
        g_b_out,
        g_scale,
    )


def solution(mesh):
    placed = (
        P("dp", ("face", "tile"), None),
        P(("face", "tile")),
        P(("face", "tile")),
        P(("face", "tile"), None),
        P(("face", "tile"), None, None),
        P(("face", "tile"), None),
        P("dp", ("face", "tile"), None),
        P(),
        P(),
        P(),
        P(),
        P(),
        P(),
        P(),
        P(),
        P(),
    )
    return jax.shard_map(
        local,
        mesh=mesh,
        in_specs=placed,
        out_specs=(
            P("dp", ("face", "tile"), None),
            P("dp", ("face", "tile"), None),
            P(),
            P(),
            P(),
            P(),
            P(),
            P(),
            P(),
            P(),
            P(),
        ),
        check_vma=False,
    )
```

profile of v0, /device:TPU:1, one launch (start us, length us, event | category | flops | bytes accessed | tf_op | source)
XLA Modules:
  0.0 182.7 jit_solution(3793223018023141763)
XLA Ops:
  3.7 5.1 %sort.17 = (s32[1024]{0:T(1024)}, s32[1024]{0:T(1024)S(1)}) sort(s32[1024]{0:T(1024)} %param.19, s32[1024]{0:T(1024)S(1)} %iota.8), dimensions={0}, to_apply=%region_0.0 | sort | flops 10240 | bytes 16384 | tf_op jit(solution)/shard_map/jit(argsort)/sort | solution.py:172
  8.8 4.5 %gather_fusion.1 = s32[1024]{0:T(1024)S(1)} fusion(s32[1024]{0:T(1024)S(1)} %copy-done.1, s32[1024]{0:T(1024)S(1)} %get-tuple-element.167), kind=kCustom, calls=%fused_computation.1 | custom fusion | bytes 12288 | tf_op jit(solution)/shard_map/gather | solution.py:174
  13.9 3.2 %gather_fusion = bf16[1024,128]{1,0:T(8,128)(2,1)S(1)} fusion(bf16[1024,128]{1,0:T(8,128)(2,1)S(1)} %bitcast.287, s32[1024]{0:T(1024)S(1)} %get-tuple-element.167), kind=kCustom, calls=%fused_computation | custom fusion | bytes 528384 | tf_op jit(solution)/shard_map/gather | solution.py:173
  18.0 16.3 %all-to-all-start = ((bf16[128,9,128]{2,1,0:T(8,128)(2,1)}), bf16[128,9,128]{2,1,0:T(8,128)(2,1)S(1)}, u32[]{:S(2)}, u32[]{:S(2)}) async-start(bf16[128,9,128]{2,1,0:T(8,128)(2,1)} %pad_maximum_fusion), calls=%async_computation | async-start | bytes 1048576 | tf_op jit(solution)/shard_map/all_to_all | solution.py:177
  34.5 16.8 %all-to-all-done = bf16[128,9,128]{2,1,0:T(8,128)(2,1)S(1)} async-done(((bf16[128,9,128]{2,1,0:T(8,128)(2,1)}), bf16[128,9,128]{2,1,0:T(8,128)(2,1)S(1)}, u32[]{:S(2)}, u32[]{:S(2)}) %all-to-all-start) | async-done | bytes 294944 | tf_op jit(solution)/shard_map/all_to_all | solution.py:177
  51.6 3.2 %scatter_custom_fusion = bf16[1024,128]{1,0:T(8,128)(2,1)S(1)} fusion(s32[1024]{0:T(1024)S(1)} %bitcast.303, bf16[128,9,128]{2,1,0:T(8,128)(2,1)S(1)} %all-to-all-done, bf16[]{:T(256)} %constant.165.clone.1), kind=kCustom, calls=%fused_computation.248 | custom fusion | bytes 524290 | tf_op jit(solution)/shard_map/scatter | solution.py:190
  54.9 1.9 %gather_fusion.2 = bf16[768,128]{1,0:T(8,128)(2,1)S(1)} fusion(bf16[1025,128]{1,0:T(8,128)(2,1)S(1)} %concatenate.98, s32[1024]{0:T(1024)S(1)} %pad_clamp_fusion.1), kind=kCustom, calls=%fused_computation.2 | custom fusion | bytes 396288 | tf_op jit(solution)/shard_map/gather | solution.py:204
  57.9 3.8 %collective-permute-start = (bf16[3,96,128]{2,1,0:T(8,128)(2,1)S(1)}, bf16[3,96,128]{2,1,0:T(8,128)(2,1)S(1)}, u32[]{:S(2)}, u32[]{:S(2)}) collective-permute-start(bf16[3,96,128]{2,1,0:T(8,128)(2,1)S(1)} %get-tuple-element.95), channel_id=1, source_target_pairs={{0,248},{8,0},{16,8},{24,16},{32,24},{40,32},{48,40},{56,48},{64,5... | collective-permute-start | bytes 221192 | tf_op jit(solution)/shard_map/ppermute | solution.py:15
  61.8 1.7 collective-permute-done.1
  63.5 2.0 %collective-permute-start.2 = (bf16[3,96,128]{2,1,0:T(8,128)(2,1)S(1)}, bf16[3,96,128]{2,1,0:T(8,128)(2,1)S(1)}, u32[]{:S(2)}, u32[]{:S(2)}) collective-permute-start(bf16[3,96,128]{2,1,0:T(8,128)(2,1)S(1)} %pad_maximum_fusion.3), channel_id=1, source_target_pairs={{0,6},{2,0},{4,2},{6,4},{1,7},{3,1},{5,3},{7,5},{8,14},{10,8},{12,... | collective-permute-start | bytes 221192 | tf_op jit(solution)/shard_map/ppermute | solution.py:15
  68.0 4.0 %collective-permute-done.3 = bf16[3,96,128]{2,1,0:T(8,128)(2,1)S(1)} collective-permute-done((bf16[3,96,128]{2,1,0:T(8,128)(2,1)S(1)}, bf16[3,96,128]{2,1,0:T(8,128)(2,1)S(1)}, u32[]{:S(2)}, u32[]{:S(2)}) %collective-permute-start.3) | collective-permute-done | bytes 73760 | tf_op jit(solution)/shard_map/ppermute | solution.py:15
  72.1 1.5 gather_fusion.3
  74.2 3.8 %add_reduce_fusion = (f32[32,32]{1,0:T(8,128)S(1)}, f32[32,32,128]{2,1,0:T(8,128)S(1)}) fusion(f32[128]{0:T(128)S(1)} %copy-done.7, f32[128]{0:T(128)S(1)} %get-tuple-element.114, f32[38,38,128]{2,1,0:T(8,128)S(1)} %maximum_convert_fusion, f32[128]{0:T(128)S(1)} %get-tuple-element.115, f32[128]{0:T(128)S(1)} %get-tuple-element.116, ...), kind=kLoop, calls=%fused_computation.237 | loop fusion | flops 12975104 | bytes 26244096 | tf_op jit(solution)/shard_map/reduce_sum | solution.py:214
  84.4 6.3 %fusion.140 = (bf16[38,38,128]{2,1,0:T(8,128)(2,1)S(1)}, f32[38,38,128]{2,1,0:T(8,128)S(1)}) fusion(f32[128]{0:T(128)S(1)} %get-tuple-element.113, f32[128]{0:T(128)S(1)} %get-tuple-element.132, f32[128]{0:T(128)S(1)} %get-tuple-element.151, f32[128]{0:T(128)S(1)} %get-tuple-element.161, f32[128]{0:T(128)S(1)} %get-tuple-element.160, ...), kind=kLoop, calls=%fused_computation.412 | loop fusion | flops 18113536 | bytes 1658368 | tf_op jit(solution)/shard_map/convert.14
  90.9 1.6 scatter_custom_fusion.1
  92.5 5.1 %collective-permute-start.5 = (bf16[3,96,128]{2,1,0:T(8,128)(2,1)S(1)}, bf16[3,96,128]{2,1,0:T(8,128)(2,1)S(1)}, u32[]{:S(2)}, u32[]{:S(2)}) collective-permute-start(bf16[3,96,128]{2,1,0:T(8,128)(2,1)S(1)} %pad_maximum_fusion.6), channel_id=1, source_target_pairs={{0,248},{8,0},{16,8},{24,16},{32,24},{40,32},{48,40},{56,48},{64,5... | collective-permute-start | bytes 221192 | tf_op jit(solution)/shard_map/ppermute | solution.py:15
  99.0 5.2 %collective-permute-done.4 = bf16[3,96,128]{2,1,0:T(8,128)(2,1)S(1)} collective-permute-done((bf16[3,96,128]{2,1,0:T(8,128)(2,1)S(1)}, bf16[3,96,128]{2,1,0:T(8,128)(2,1)S(1)}, u32[]{:S(2)}, u32[]{:S(2)}) %collective-permute-start.4) | collective-permute-done | bytes 73760 | tf_op jit(solution)/shard_map/ppermute | solution.py:15
  104.8 4.0 %collective-permute-done.6 = bf16[3,96,128]{2,1,0:T(8,128)(2,1)S(1)} collective-permute-done((bf16[3,96,128]{2,1,0:T(8,128)(2,1)S(1)}, bf16[3,96,128]{2,1,0:T(8,128)(2,1)S(1)}, u32[]{:S(2)}, u32[]{:S(2)}) %collective-permute-start.6) | collective-permute-done | bytes 73760 | tf_op jit(solution)/shard_map/ppermute | solution.py:15
  109.4 2.6 %collective-permute-done.7 = bf16[3,96,128]{2,1,0:T(8,128)(2,1)S(1)} collective-permute-done((bf16[3,96,128]{2,1,0:T(8,128)(2,1)S(1)}, bf16[3,96,128]{2,1,0:T(8,128)(2,1)S(1)}, u32[]{:S(2)}, u32[]{:S(2)}) %collective-permute-start.7) | collective-permute-done | bytes 73760 | tf_op jit(solution)/shard_map/ppermute | solution.py:15
  112.3 6.5 %scatter_custom_fusion.2 = f32[1025,128]{1,0:T(8,128)S(1)} fusion(s32[768]{0:T(1024)S(1)} %fusion.132, bf16[768,128]{1,0:T(8,128)(2,1)S(1)} %bitcast_select_fusion, f32[]{:T(128)} %constant.184.clone.1), kind=kCustom, calls=%fused_computation.239 | custom fusion | flops 196608 | bytes 721412 | tf_op jit(solution)/shard_map/scatter-add | solution.py:263
  120.1 10.5 %collective-permute-start.8 = (f32[36352]{0:T(1024)S(1)}, f32[36352]{0:T(1024)S(1)}, u32[]{:S(2)}, u32[]{:S(2)}) collective-permute-start(f32[36352]{0:T(1024)S(1)} %slice_select_fusion), channel_id=1, source_target_pairs={{0,1},{1,0},{2,3},{3,2},{4,5},{5,4},{6,7},{7,6},{8,9},{9,8},{10,11... | collective-permute-start | bytes 436232 | tf_op jit(solution)/shard_map/ppermute | solution.py:42
  131.7 3.2 %collective-permute-done.9 = f32[18176]{0:T(1024)S(1)} collective-permute-done((f32[18176]{0:T(1024)S(1)}, f32[18176]{0:T(1024)S(1)}, u32[]{:S(2)}, u32[]{:S(2)}) %collective-permute-start.9) | collective-permute-done | bytes 72736 | tf_op jit(solution)/shard_map/ppermute | solution.py:42
  136.2 3.1 %collective-permute-done.10 = f32[9088]{0:T(1024)S(1)} collective-permute-done((f32[9088]{0:T(1024)S(1)}, f32[9088]{0:T(1024)S(1)}, u32[]{:S(2)}, u32[]{:S(2)}) %collective-permute-start.10) | collective-permute-done | bytes 36384 | tf_op jit(solution)/shard_map/ppermute | solution.py:42
  139.5 2.8 %collective-permute-done.11 = f32[9088]{0:T(1024)S(1)} collective-permute-done((f32[9088]{0:T(1024)S(1)}, f32[9088]{0:T(1024)S(1)}, u32[]{:S(2)}, u32[]{:S(2)}) %collective-permute-start.11) | collective-permute-done | bytes 36384 | tf_op jit(solution)/shard_map/ppermute | solution.py:44
  142.3 3.8 %collective-permute-done.12 = f32[9088]{0:T(1024)S(1)} collective-permute-done((f32[9088]{0:T(1024)S(1)}, f32[9088]{0:T(1024)S(1)}, u32[]{:S(2)}, u32[]{:S(2)}) %collective-permute-start.12) | collective-permute-done | bytes 36384 | tf_op jit(solution)/shard_map/ppermute | solution.py:44
  146.1 6.7 %collective-permute-done.13 = f32[9088]{0:T(1024)S(1)} collective-permute-done((f32[9088]{0:T(1024)S(1)}, f32[9088]{0:T(1024)S(1)}, u32[]{:S(2)}, u32[]{:S(2)}) %collective-permute-start.13) | collective-permute-done | bytes 36384 | tf_op jit(solution)/shard_map/ppermute | solution.py:44
  152.8 2.8 %collective-permute-done.14 = f32[9088]{0:T(1024)S(1)} collective-permute-done((f32[9088]{0:T(1024)S(1)}, f32[9088]{0:T(1024)S(1)}, u32[]{:S(2)}, u32[]{:S(2)}) %collective-permute-start.14) | collective-permute-done | bytes 36384 | tf_op jit(solution)/shard_map/ppermute | solution.py:44
  155.6 4.3 %collective-permute-done.15 = f32[9088]{0:T(1024)S(1)} collective-permute-done((f32[9088]{0:T(1024)S(1)}, f32[9088]{0:T(1024)S(1)}, u32[]{:S(2)}, u32[]{:S(2)}) %collective-permute-start.15) | collective-permute-done | bytes 36384 | tf_op jit(solution)/shard_map/ppermute | solution.py:44
  159.9 1.5 collective-permute-start.16
  161.4 2.8 %collective-permute-done.16 = f32[9088]{0:T(1024)S(1)} collective-permute-done((f32[9088]{0:T(1024)S(1)}, f32[9088]{0:T(1024)S(1)}, u32[]{:S(2)}, u32[]{:S(2)}) %collective-permute-start.16) | collective-permute-done | bytes 36384 | tf_op jit(solution)/shard_map/ppermute | solution.py:48
  165.2 2.6 %collective-permute-done.17 = f32[18176]{0:T(1024)S(1)} collective-permute-done((f32[18176]{0:T(1024)S(1)}, f32[18176]{0:T(1024)S(1)}, u32[]{:S(2)}, u32[]{:S(2)}) %collective-permute-start.17) | collective-permute-done | bytes 72736 | tf_op jit(solution)/shard_map/ppermute | solution.py:48
  167.9 10.6 %collective-permute-start.18 = (f32[36352]{0:T(1024)S(1)}, f32[36352]{0:T(1024)S(1)}, u32[]{:S(2)}, u32[]{:S(2)}) collective-permute-start(f32[36352]{0:T(1024)S(1)} %maximum_select_fusion.2), channel_id=1, source_target_pairs={{0,1},{1,0},{2,3},{3,2},{4,5},{5,4},{6,7},{7,6},{8,9},{9,8},{10,11... | collective-permute-start | bytes 436232 | tf_op jit(solution)/shard_map/ppermute | solution.py:48
  (187 shorter events, 27.4 us)
Async XLA Ops:
  0.6 13.2 %copy-start = (bf16[1,1024,128]{2,1,0:T(8,128)(2,1)S(1)}, bf16[1,1024,128]{2,1,0:T(8,128)(2,1)}, u32[]{:S(2)}) copy-start(bf16[1,1024,128]{2,1,0:T(8,128)(2,1)} %param.18) | copy-start | bytes 786436
  0.7 8.1 %copy-start.1 = (s32[1024]{0:T(1024)S(1)}, s32[1024]{0:T(1024)}, u32[]{:S(2)}) copy-start(s32[1024]{0:T(1024)} %param.20) | copy-start | bytes 12292
  17.1 17.3 %copy-start.5 = (s32[1,8,96]{2,1,0:T(8,128)S(1)}, s32[1,8,96]{2,1,0:T(8,128)}, u32[]{:S(2)}) copy-start(s32[1,8,96]{2,1,0:T(8,128)} %param.22) | copy-start | bytes 9220
  17.1 17.3 %copy-start.13 = (s32[1,8]{1,0:T(1,128)S(1)}, s32[1,8]{1,0:T(1,128)}, u32[]{:S(2)}) copy-start(s32[1,8]{1,0:T(1,128)} %param.21) | copy-start | bytes 100
  17.1 17.4 %copy-start.6 = (bf16[49,128]{1,0:T(8,128)(2,1)S(1)}, bf16[49,128]{1,0:T(8,128)(2,1)}, u32[]{:S(2)}) copy-start(bf16[49,128]{1,0:T(8,128)(2,1)} %param.25) | copy-start | bytes 37636
  18.0 33.4 %all-to-all-start = ((bf16[128,9,128]{2,1,0:T(8,128)(2,1)}), bf16[128,9,128]{2,1,0:T(8,128)(2,1)S(1)}, u32[]{:S(2)}, u32[]{:S(2)}) async-start(bf16[128,9,128]{2,1,0:T(8,128)(2,1)} %pad_maximum_fusion), calls=%async_computation | async-start | bytes 1048576 | tf_op jit(solution)/shard_map/all_to_all | solution.py:177
  56.9 6.6 %collective-permute-start.1 = (bf16[3,96,128]{2,1,0:T(8,128)(2,1)S(1)}, bf16[3,96,128]{2,1,0:T(8,128)(2,1)S(1)}, u32[]{:S(2)}, u32[]{:S(2)}) collective-permute-start(bf16[3,96,128]{2,1,0:T(8,128)(2,1)S(1)} %get-tuple-element.96), channel_id=1, source_target_pairs={{0,8},{8,16},{16,24},{24,32},{32,40},{40,48},{48,56},{56,64},{64,7... | collective-permute-start | bytes 221192 | tf_op jit(solution)/shard_map/ppermute | solution.py:15
  57.9 5.6 %collective-permute-start = (bf16[3,96,128]{2,1,0:T(8,128)(2,1)S(1)}, bf16[3,96,128]{2,1,0:T(8,128)(2,1)S(1)}, u32[]{:S(2)}, u32[]{:S(2)}) collective-permute-start(bf16[3,96,128]{2,1,0:T(8,128)(2,1)S(1)} %get-tuple-element.95), channel_id=1, source_target_pairs={{0,248},{8,0},{16,8},{24,16},{32,24},{40,32},{48,40},{56,48},{64,5... | collective-permute-start | bytes 221192 | tf_op jit(solution)/shard_map/ppermute | solution.py:15
  63.5 3.6 %collective-permute-start.2 = (bf16[3,96,128]{2,1,0:T(8,128)(2,1)S(1)}, bf16[3,96,128]{2,1,0:T(8,128)(2,1)S(1)}, u32[]{:S(2)}, u32[]{:S(2)}) collective-permute-start(bf16[3,96,128]{2,1,0:T(8,128)(2,1)S(1)} %pad_maximum_fusion.3), channel_id=1, source_target_pairs={{0,6},{2,0},{4,2},{6,4},{1,7},{3,1},{5,3},{7,5},{8,14},{10,8},{12,... | collective-permute-start | bytes 221192 | tf_op jit(solution)/shard_map/ppermute | solution.py:15
  67.1 4.8 %collective-permute-start.3 = (bf16[3,96,128]{2,1,0:T(8,128)(2,1)S(1)}, bf16[3,96,128]{2,1,0:T(8,128)(2,1)S(1)}, u32[]{:S(2)}, u32[]{:S(2)}) collective-permute-start(bf16[3,96,128]{2,1,0:T(8,128)(2,1)S(1)} %pad_maximum_fusion.4), channel_id=1, source_target_pairs={{0,2},{2,4},{4,6},{6,0},{1,3},{3,5},{5,7},{7,1},{8,10},{10,12},{12... | collective-permute-start | bytes 221192 | tf_op jit(solution)/shard_map/ppermute | solution.py:15
  78.0 0.9 copy-start.8
  78.0 0.9 copy-start.9
  78.0 0.9 copy-start.11
  78.9 1.0 copy-start.2
  78.9 0.9 copy-start.4
  78.9 0.9 copy-start.10
  92.5 6.5 %collective-permute-start.5 = (bf16[3,96,128]{2,1,0:T(8,128)(2,1)S(1)}, bf16[3,96,128]{2,1,0:T(8,128)(2,1)S(1)}, u32[]{:S(2)}, u32[]{:S(2)}) collective-permute-start(bf16[3,96,128]{2,1,0:T(8,128)(2,1)S(1)} %pad_maximum_fusion.6), channel_id=1, source_target_pairs={{0,248},{8,0},{16,8},{24,16},{32,24},{40,32},{48,40},{56,48},{64,5... | collective-permute-start | bytes 221192 | tf_op jit(solution)/shard_map/ppermute | solution.py:15
  97.6 6.6 %collective-permute-start.4 = (bf16[3,96,128]{2,1,0:T(8,128)(2,1)S(1)}, bf16[3,96,128]{2,1,0:T(8,128)(2,1)S(1)}, u32[]{:S(2)}, u32[]{:S(2)}) collective-permute-start(bf16[3,96,128]{2,1,0:T(8,128)(2,1)S(1)} %pad_maximum_fusion.5), channel_id=1, source_target_pairs={{0,8},{8,16},{16,24},{24,32},{32,40},{40,48},{48,56},{56,64},{64,7... | collective-permute-start | bytes 221192 | tf_op jit(solution)/shard_map/ppermute | solution.py:15
  104.2 4.5 %collective-permute-start.6 = (bf16[3,96,128]{2,1,0:T(8,128)(2,1)S(1)}, bf16[3,96,128]{2,1,0:T(8,128)(2,1)S(1)}, u32[]{:S(2)}, u32[]{:S(2)}) collective-permute-start(bf16[3,96,128]{2,1,0:T(8,128)(2,1)S(1)} %pad_maximum_fusion.7), channel_id=1, source_target_pairs={{0,2},{2,4},{4,6},{6,0},{1,3},{3,5},{5,7},{7,1},{8,10},{10,12},{12... | collective-permute-start | bytes 221192 | tf_op jit(solution)/shard_map/ppermute | solution.py:15
  104.7 14.1 %copy-start.12 = (f32[128]{0:T(128)S(1)}, f32[128]{0:T(128)}, u32[]{:S(2)}) copy-start(f32[128]{0:T(128)} %param.32) | copy-start | bytes 1540
  108.8 3.3 %collective-permute-start.7 = (bf16[3,96,128]{2,1,0:T(8,128)(2,1)S(1)}, bf16[3,96,128]{2,1,0:T(8,128)(2,1)S(1)}, u32[]{:S(2)}, u32[]{:S(2)}) collective-permute-start(bf16[3,96,128]{2,1,0:T(8,128)(2,1)S(1)} %pad_maximum_fusion.8), channel_id=1, source_target_pairs={{0,6},{2,0},{4,2},{6,4},{1,7},{3,1},{5,3},{7,5},{8,14},{10,8},{12,... | collective-permute-start | bytes 221192 | tf_op jit(solution)/shard_map/ppermute | solution.py:15
  120.1 11.5 %collective-permute-start.8 = (f32[36352]{0:T(1024)S(1)}, f32[36352]{0:T(1024)S(1)}, u32[]{:S(2)}, u32[]{:S(2)}) collective-permute-start(f32[36352]{0:T(1024)S(1)} %slice_select_fusion), channel_id=1, source_target_pairs={{0,1},{1,0},{2,3},{3,2},{4,5},{5,4},{6,7},{7,6},{8,9},{9,8},{10,11... | collective-permute-start | bytes 436232 | tf_op jit(solution)/shard_map/ppermute | solution.py:42
  131.6 3.3 %collective-permute-start.9 = (f32[18176]{0:T(1024)S(1)}, f32[18176]{0:T(1024)S(1)}, u32[]{:S(2)}, u32[]{:S(2)}) collective-permute-start(f32[18176]{0:T(1024)S(1)} %slice_select_fusion.1), channel_id=1, source_target_pairs={{0,2},{2,0},{4,6},{6,4},{1,3},{3,1},{5,7},{7,5},{8,10},{10,8},{12,... | collective-permute-start | bytes 218120 | tf_op jit(solution)/shard_map/ppermute | solution.py:42
  134.9 4.4 %collective-permute-start.10 = (f32[9088]{0:T(1024)S(1)}, f32[9088]{0:T(1024)S(1)}, u32[]{:S(2)}, u32[]{:S(2)}) collective-permute-start(f32[9088]{0:T(1024)S(1)} %slice_select_fusion.2), channel_id=1, source_target_pairs={{0,4},{2,6},{4,0},{6,2},{1,5},{3,7},{5,1},{7,3},{8,12},{10,14},{12... | collective-permute-start | bytes 109064 | tf_op jit(solution)/shard_map/ppermute | solution.py:42
  139.3 2.9 %collective-permute-start.11 = (f32[9088]{0:T(1024)S(1)}, f32[9088]{0:T(1024)S(1)}, u32[]{:S(2)}, u32[]{:S(2)}) collective-permute-start(f32[9088]{0:T(1024)S(1)} %select_add_fusion.2), channel_id=1, source_target_pairs={{0,8},{8,0},{16,24},{24,16},{32,40},{40,32},{48,56},{56,48},{64,72... | collective-permute-start | bytes 109064 | tf_op jit(solution)/shard_map/ppermute | solution.py:44
  142.3 3.8 %collective-permute-start.12 = (f32[9088]{0:T(1024)S(1)}, f32[9088]{0:T(1024)S(1)}, u32[]{:S(2)}, u32[]{:S(2)}) collective-permute-start(f32[9088]{0:T(1024)S(1)} %add.642), channel_id=1, source_target_pairs={{0,16},{8,24},{16,0},{24,8},{32,48},{40,56},{48,32},{56,40},{64,80... | collective-permute-start | bytes 109064 | tf_op jit(solution)/shard_map/ppermute | solution.py:44
  146.1 6.7 %collective-permute-start.13 = (f32[9088]{0:T(1024)S(1)}, f32[9088]{0:T(1024)S(1)}, u32[]{:S(2)}, u32[]{:S(2)}) collective-permute-start(f32[9088]{0:T(1024)S(1)} %add.643), channel_id=1, source_target_pairs={{0,32},{8,40},{16,48},{24,56},{32,0},{40,8},{48,16},{56,24},{64,96... | collective-permute-start | bytes 109064 | tf_op jit(solution)/shard_map/ppermute | solution.py:44
  152.8 2.8 %collective-permute-start.14 = (f32[9088]{0:T(1024)S(1)}, f32[9088]{0:T(1024)S(1)}, u32[]{:S(2)}, u32[]{:S(2)}) collective-permute-start(f32[9088]{0:T(1024)S(1)} %add.644), channel_id=1, source_target_pairs={{0,64},{8,72},{16,80},{24,88},{32,96},{40,104},{48,112},{56,120},{... | collective-permute-start | bytes 109064 | tf_op jit(solution)/shard_map/ppermute | solution.py:44
  155.6 4.3 %collective-permute-start.15 = (f32[9088]{0:T(1024)S(1)}, f32[9088]{0:T(1024)S(1)}, u32[]{:S(2)}, u32[]{:S(2)}) collective-permute-start(f32[9088]{0:T(1024)S(1)} %add.645), channel_id=1, source_target_pairs={{0,128},{8,136},{16,144},{24,152},{32,160},{40,168},{48,176},{56,1... | collective-permute-start | bytes 109064 | tf_op jit(solution)/shard_map/ppermute | solution.py:44
  159.9 4.3 %collective-permute-start.16 = (f32[9088]{0:T(1024)S(1)}, f32[9088]{0:T(1024)S(1)}, u32[]{:S(2)}, u32[]{:S(2)}) collective-permute-start(f32[9088]{0:T(1024)S(1)} %add.646), channel_id=1, source_target_pairs={{0,4},{2,6},{4,0},{6,2},{1,5},{3,7},{5,1},{7,3},{8,12},{10,14},{12... | collective-permute-start | bytes 109064 | tf_op jit(solution)/shard_map/ppermute | solution.py:48
  164.3 3.6 %collective-permute-start.17 = (f32[18176]{0:T(1024)S(1)}, f32[18176]{0:T(1024)S(1)}, u32[]{:S(2)}, u32[]{:S(2)}) collective-permute-start(f32[18176]{0:T(1024)S(1)} %maximum_select_fusion.5), channel_id=1, source_target_pairs={{0,2},{2,0},{4,6},{6,4},{1,3},{3,1},{5,7},{7,5},{8,10},{10,8},{12,... | collective-permute-start | bytes 218120 | tf_op jit(solution)/shard_map/ppermute | solution.py:48
  167.9 11.6 %collective-permute-start.18 = (f32[36352]{0:T(1024)S(1)}, f32[36352]{0:T(1024)S(1)}, u32[]{:S(2)}, u32[]{:S(2)}) collective-permute-start(f32[36352]{0:T(1024)S(1)} %maximum_select_fusion.2), channel_id=1, source_target_pairs={{0,1},{1,0},{2,3},{3,2},{4,5},{5,4},{6,7},{7,6},{8,9},{9,8},{10,11... | collective-permute-start | bytes 436232 | tf_op jit(solution)/shard_map/ppermute | solution.py:48
  (2 other events, 1.6 us)
where the time goes:
time: 183 us
  waiting for transfers between devices  70.8 us (39%)
  starting transfers between devices  54.8 us (30%)
  other arithmetic  32.7 us (18%)
  local copies, waits for them, and re-layouts  19.5 us (11%)
  matrix products  3.32 us (2%)
    ppermute x5, waiting for transfers between devices, tree_sum(): buf = buf + lax.ppermute(buf, axis, [(i, i ^ bit) for i in range(size)])  20.4 us
    ppermute x8, waiting for transfers between devices, from_behind(): return lax.ppermute(value, axis, pairs)  19.9 us
    all_to_all x1, waiting for transfers between devices, local(): lax.all_to_all(jnp.concatenate([outgoing, label_row], axis=1), ('face', '...  16.8 us
    all_to_all x1, starting transfers between devices, local(): lax.all_to_all(jnp.concatenate([outgoing, label_row], axis=1), ('face', '...  16.3 us
    ppermute x8, starting transfers between devices, from_behind(): return lax.ppermute(value, axis, pairs)  13.5 us
    ppermute x3, starting transfers between devices, tree_sum(): got = lax.ppermute(buf, axis, pairs)  13 us
    ppermute x3, starting transfers between devices, tree_sum(): buf = keep + lax.ppermute(send, axis, pairs)  11.8 us
    ppermute x3, waiting for transfers between devices, tree_sum(): buf = keep + lax.ppermute(send, axis, pairs)  7.3 us
  transfers between devices with their start and end apart: 20, of which 19 were waited for; matrix products, arithmetic and copies ran while one was open for 1% of the time, Pallas kernels for 0%

commit v1 on v0

--- a/solution.py
+++ b/solution.py
@@ -15,7 +15,7 @@
     return lax.ppermute(value, axis, pairs)
 
 
-def tree_sum(parts, halving_axes, doubling_axes):
+def tree_sum(parts, halving_axes, doubling_axes, rider=None, stages=()):
     flat = jnp.concatenate([part.reshape(-1) for part in parts])
 
     def bits_of(axes):
@@ -29,6 +29,17 @@
         return steps
 
     halving = bits_of(halving_axes)
+    plan = dict(stages)
+    count = [0]
+
+    def stepped(buf):
+        nonlocal rider
+        count[0] += 1
+        if count[0] in plan:
+            buf, rider = lax.optimization_barrier((buf, rider))
+            rider = plan[count[0]](rider)
+        return buf
+
     total = flat.shape[0]
     pad = (-total) % (1 << len(halving))
     buf = jnp.pad(flat, (0, pad))
@@ -39,20 +50,20 @@
         keep = jnp.where(upper, high, low)
         send = jnp.where(upper, low, high)
         pairs = [(i, i ^ bit) for i in range(size)]
-        buf = keep + lax.ppermute(send, axis, pairs)
+        buf = stepped(keep + lax.ppermute(send, axis, pairs))
     for axis, bit, size in bits_of(doubling_axes):
-        buf = buf + lax.ppermute(buf, axis, [(i, i ^ bit) for i in range(size)])
+        buf = stepped(buf + lax.ppermute(buf, axis, [(i, i ^ bit) for i in range(size)]))
     for axis, bit, size in reversed(halving):
         upper = (lax.axis_index(axis) // bit) % 2 == 1
         pairs = [(i, i ^ bit) for i in range(size)]
         got = lax.ppermute(buf, axis, pairs)
-        buf = jnp.where(upper, jnp.concatenate([got, buf]), jnp.concatenate([buf, got]))
+        buf = stepped(jnp.where(upper, jnp.concatenate([got, buf]), jnp.concatenate([buf, got])))
     out = []
     start = 0
     for part in parts:
         out.append(buf[start : start + part.size].reshape(part.shape))
         start += part.size
-    return tuple(out)
+    return tuple(out), rider
 
 def cycle_cells(tile_side):
     padded_side = tile_side + 6
@@ -124,21 +135,19 @@
     return 0.5 * (1.0 + lax.erf(values * 0.7071067811865476))
 
 
-def move_links(blocks, heading):
-    ups = [k for k, offset in enumerate(LINK_OFFSETS) if offset[0] == -1]
-    downs = [k for k, offset in enumerate(LINK_OFFSETS) if offset[0] == 1]
+def move_round(blocks, heading, axis):
+    along = 0 if axis == "face" else 1
     moved = list(blocks[k] for k in range(len(LINK_OFFSETS)))
-    for group, step in ((ups, -heading), (downs, heading)):
-        shifted = from_behind(jnp.stack([moved[k] for k in group]), "face", step)
-        for place, k in enumerate(group):
-            moved[k] = shifted[place]
-    lefts = [k for k, offset in enumerate(LINK_OFFSETS) if offset[1] == -1]
-    rights = [k for k, offset in enumerate(LINK_OFFSETS) if offset[1] == 1]
-    for group, step in ((lefts, -heading), (rights, heading)):
-        shifted = from_behind(jnp.stack([moved[k] for k in group]), "tile", step)
+    for sign in (-1, 1):
+        group = [k for k, offset in enumerate(LINK_OFFSETS) if offset[along] == sign]
+        shifted = from_behind(jnp.stack([moved[k] for k in group]), axis, sign * heading)
         for place, k in enumerate(group):
             moved[k] = shifted[place]
     return jnp.stack(moved)
+
+
+def move_links(blocks, heading):
+    return move_round(move_round(blocks, heading, "face"), heading, "tile")
 
 
 def local(
@@ -255,19 +264,28 @@
         jnp.zeros((8 * capacity + 1, channels), jnp.bfloat16).at[recv_index].set(cycle_grad)
     )
     back_parcel = back_parcel[: 8 * capacity].reshape(8, capacity, channels)
-    returned = move_links(back_parcel, -1)
-    returned = jnp.where(live, returned, jnp.zeros((), returned.dtype))
-    incoming = (
-        jnp.zeros((pixel_count + 1, channels), jnp.float32)
-        .at[send_pixels[0].reshape(-1)]
-        .add(returned.reshape(-1, channels).astype(jnp.float32))
-    )
-    field_grad = (grad_f + inner_grad + incoming[:pixel_count]).astype(jnp.bfloat16)
-    g_kern, g_cbias, g_gain, g_nbias, g_w_in, g_b_in, g_w_out, g_b_out, g_scale = tree_sum(
+
+    def finish(moved):
+        returned = jnp.where(live, moved, jnp.zeros((), moved.dtype))
+        incoming = (
+            jnp.zeros((pixel_count + 1, channels), jnp.float32)
+            .at[send_pixels[0].reshape(-1)]
+            .add(returned.reshape(-1, channels).astype(jnp.float32))
+        )
+        return (grad_f + inner_grad + incoming[:pixel_count]).astype(jnp.bfloat16)
+
+    sums, field_grad = tree_sum(
         (g_kern, g_cbias, g_gain, g_nbias, g_w_in, g_b_in, g_w_out, g_b_out, g_scale),
         ("dp", "tile"),
         ("face",),
-    )
+        rider=back_parcel,
+        stages=(
+            (1, lambda parcel: move_round(parcel, -1, "face")),
+            (3, lambda parcel: move_round(parcel, -1, "tile")),
+            (5, finish),
+        ),
+    )
+    g_kern, g_cbias, g_gain, g_nbias, g_w_in, g_b_in, g_w_out, g_b_out, g_scale = sums
     return (
         block_out[None],
         field_grad[None],

time: 183 us -> 162 us (0.89)
  waiting for transfers between devices: 70.8 us -> 52.6 us
  starting transfers between devices: 54.8 us -> 52.2 us
    ppermute x8, waiting for transfers between devices: 27.7 us -> 16.2 us  [the longest x5 16.2 us: tree_sum(): lax.ppermute(buf, axis, [(i, i ^ bit) for i in range(size)])]
    ppermute x8, waiting for transfers between devices: 19.9 us -> 14.7 us  [from_behind(): return lax.ppermute(value, axis, pairs)]
    ppermute x8, starting transfers between devices: 11.9 us -> 8.98 us  [the longest x3 8.78 us: tree_sum(): buf = stepped(keep + lax.ppermute(send, axis, pairs))]
    another operation x9 -> x8, other arithmetic: 6.34 us -> 6.23 us
  transfers between devices with their start and end apart: 20 -> 20, of which waited for: 19 -> 13; matrix products, arithmetic and copies ran while one was open for 1% -> 10% of each run, Pallas kernels for 0% -> 0%
where the time goes in v1:
time: 162 us
  waiting for transfers between devices  52.6 us (32%)
  starting transfers between devices  52.2 us (32%)
  other arithmetic  33.2 us (20%)
  local copies, waits for them, and re-layouts  19.4 us (12%)
  matrix products  3.21 us (2%)
    all_to_all x1, waiting for transfers between devices, local(): lax.all_to_all(jnp.concatenate([outgoing, label_row], axis=1), ('face', '...  16.8 us
    all_to_all x1, starting transfers between devices, local(): lax.all_to_all(jnp.concatenate([outgoing, label_row], axis=1), ('face', '...  16.3 us
    ppermute x5, waiting for transfers between devices, tree_sum(): lax.ppermute(buf, axis, [(i, i ^ bit) for i in range(size)])  16.2 us
    ppermute x8, waiting for transfers between devices, from_behind(): return lax.ppermute(value, axis, pairs)  14.7 us
    ppermute x8, starting transfers between devices, from_behind(): return lax.ppermute(value, axis, pairs)  14.4 us
    ppermute x3, starting transfers between devices, tree_sum(): got = lax.ppermute(buf, axis, pairs)  12.5 us
    ppermute x3, starting transfers between devices, tree_sum(): buf = stepped(keep + lax.ppermute(send, axis, pairs))  8.78 us
    scatter-add x1, other arithmetic, finish(): incoming = jnp.zeros((pixel_count + 1, channels), jnp.float32).at[send_pi...  6.52 us
  transfers between devices with their start and end apart: 20, of which 13 were waited for; matrix products, arithmetic and copies ran while one was open for 10% of the time, Pallas kernels for 0%

profile of v1, /device:TPU:1, one launch (start us, length us, event | category | flops | bytes accessed | tf_op | source)
XLA Modules:
  0.0 162.2 jit_solution(17535069356587018961)
XLA Ops:
  3.0 5.1 %sort.17 = (s32[1024]{0:T(1024)}, s32[1024]{0:T(1024)S(1)}) sort(s32[1024]{0:T(1024)} %param.19, s32[1024]{0:T(1024)S(1)} %iota.8), dimensions={0}, to_apply=%region_0.0 | sort | flops 10240 | bytes 16384 | tf_op jit(solution)/shard_map/jit(argsort)/sort | solution.py:181
  8.8 4.5 %gather_fusion.1 = s32[1024]{0:T(1024)S(1)} fusion(s32[1024]{0:T(1024)S(1)} %copy-done.1, s32[1024]{0:T(1024)S(1)} %get-tuple-element.175), kind=kCustom, calls=%fused_computation.1 | custom fusion | bytes 12288 | tf_op jit(solution)/shard_map/gather | solution.py:183
  13.9 3.2 %gather_fusion = bf16[1024,128]{1,0:T(8,128)(2,1)S(1)} fusion(bf16[1024,128]{1,0:T(8,128)(2,1)S(1)} %bitcast.272, s32[1024]{0:T(1024)S(1)} %get-tuple-element.175), kind=kCustom, calls=%fused_computation | custom fusion | bytes 528384 | tf_op jit(solution)/shard_map/gather | solution.py:182
  18.0 16.3 %all-to-all-start = ((bf16[128,9,128]{2,1,0:T(8,128)(2,1)}), bf16[128,9,128]{2,1,0:T(8,128)(2,1)S(1)}, u32[]{:S(2)}, u32[]{:S(2)}) async-start(bf16[128,9,128]{2,1,0:T(8,128)(2,1)} %pad_maximum_fusion), calls=%async_computation | async-start | bytes 1048576 | tf_op jit(solution)/shard_map/all_to_all | solution.py:186
  34.5 16.8 %all-to-all-done = bf16[128,9,128]{2,1,0:T(8,128)(2,1)S(1)} async-done(((bf16[128,9,128]{2,1,0:T(8,128)(2,1)}), bf16[128,9,128]{2,1,0:T(8,128)(2,1)S(1)}, u32[]{:S(2)}, u32[]{:S(2)}) %all-to-all-start) | async-done | bytes 294944 | tf_op jit(solution)/shard_map/all_to_all | solution.py:186
  51.6 3.2 %scatter_custom_fusion = bf16[1024,128]{1,0:T(8,128)(2,1)S(1)} fusion(s32[1024]{0:T(1024)S(1)} %bitcast.291, bf16[128,9,128]{2,1,0:T(8,128)(2,1)S(1)} %all-to-all-done, bf16[]{:T(256)} %constant.165.clone.1), kind=kCustom, calls=%fused_computation.248 | custom fusion | bytes 524290 | tf_op jit(solution)/shard_map/scatter | solution.py:199
  54.9 1.9 %gather_fusion.2 = bf16[768,128]{1,0:T(8,128)(2,1)S(1)} fusion(bf16[1025,128]{1,0:T(8,128)(2,1)S(1)} %concatenate.98, s32[1024]{0:T(1024)S(1)} %pad_clamp_fusion.1), kind=kCustom, calls=%fused_computation.2 | custom fusion | bytes 396288 | tf_op jit(solution)/shard_map/gather | solution.py:213
  57.9 3.8 %collective-permute-start = (bf16[3,96,128]{2,1,0:T(8,128)(2,1)S(1)}, bf16[3,96,128]{2,1,0:T(8,128)(2,1)S(1)}, u32[]{:S(2)}, u32[]{:S(2)}) collective-permute-start(bf16[3,96,128]{2,1,0:T(8,128)(2,1)S(1)} %get-tuple-element.107), channel_id=1, source_target_pairs={{0,248},{8,0},{16,8},{24,16},{32,24},{40,32},{48,40},{56,48},{64,5... | collective-permute-start | bytes 221192 | tf_op jit(solution)/shard_map/ppermute | solution.py:15
  61.8 1.7 %collective-permute-done.1 = bf16[3,96,128]{2,1,0:T(8,128)(2,1)S(1)} collective-permute-done((bf16[3,96,128]{2,1,0:T(8,128)(2,1)S(1)}, bf16[3,96,128]{2,1,0:T(8,128)(2,1)S(1)}, u32[]{:S(2)}, u32[]{:S(2)}) %collective-permute-start.1) | collective-permute-done | bytes 73760 | tf_op jit(solution)/shard_map/ppermute | solution.py:15
  63.5 2.0 %collective-permute-start.2 = (bf16[3,96,128]{2,1,0:T(8,128)(2,1)S(1)}, bf16[3,96,128]{2,1,0:T(8,128)(2,1)S(1)}, u32[]{:S(2)}, u32[]{:S(2)}) collective-permute-start(bf16[3,96,128]{2,1,0:T(8,128)(2,1)S(1)} %pad_maximum_fusion.4), channel_id=1, source_target_pairs={{0,6},{2,0},{4,2},{6,4},{1,7},{3,1},{5,3},{7,5},{8,14},{10,8},{12,... | collective-permute-start | bytes 221192 | tf_op jit(solution)/shard_map/ppermute | solution.py:15
  65.5 1.6 collective-permute-done.2
  68.0 4.0 %collective-permute-done.3 = bf16[3,96,128]{2,1,0:T(8,128)(2,1)S(1)} collective-permute-done((bf16[3,96,128]{2,1,0:T(8,128)(2,1)S(1)}, bf16[3,96,128]{2,1,0:T(8,128)(2,1)S(1)}, u32[]{:S(2)}, u32[]{:S(2)}) %collective-permute-start.3) | collective-permute-done | bytes 73760 | tf_op jit(solution)/shard_map/ppermute | solution.py:15
  72.1 1.5 gather_fusion.3
  74.2 3.8 %add_reduce_fusion = (f32[32,32]{1,0:T(8,128)S(1)}, f32[32,32,128]{2,1,0:T(8,128)S(1)}) fusion(f32[128]{0:T(128)S(1)} %copy-done.6, f32[128]{0:T(128)S(1)} %get-tuple-element.122, f32[38,38,128]{2,1,0:T(8,128)S(1)} %maximum_convert_fusion, f32[128]{0:T(128)S(1)} %get-tuple-element.123, f32[128]{0:T(128)S(1)} %get-tuple-element.124, ...), kind=kLoop, calls=%fused_computation.237 | loop fusion | flops 12975104 | bytes 26244096 | tf_op jit(solution)/shard_map/reduce_sum | solution.py:223
  86.2 6.7 %collective-permute-start.4 = (f32[36352]{0:T(1024)S(1)}, f32[36352]{0:T(1024)S(1)}, u32[]{:S(2)}, u32[]{:S(2)}) collective-permute-start(f32[36352]{0:T(1024)S(1)} %slice_select_fusion), channel_id=1, source_target_pairs={{0,1},{1,0},{2,3},{3,2},{4,5},{5,4},{6,7},{7,6},{8,9},{9,8},{10,11... | collective-permute-start | bytes 436232 | tf_op jit(solution)/shard_map/ppermute | solution.py:53
  92.9 6.1 %fusion.138 = (bf16[38,38,128]{2,1,0:T(8,128)(2,1)S(1)}, f32[38,38,128]{2,1,0:T(8,128)S(1)}) fusion(f32[128]{0:T(128)S(1)} %get-tuple-element.121, f32[128]{0:T(128)S(1)} %get-tuple-element.140, f32[128]{0:T(128)S(1)} %get-tuple-element.159, f32[128]{0:T(128)S(1)} %get-tuple-element.169, f32[128]{0:T(128)S(1)} %get-tuple-element.168, ...), kind=kLoop, calls=%fused_computation.402 | loop fusion | flops 18113536 | bytes 1658368 | tf_op jit(solution)/shard_map/convert.15
  99.2 1.6 %scatter_custom_fusion.1 = bf16[769,128]{1,0:T(8,128)(2,1)S(1)} fusion(s32[420]{0:T(512)S(1)} %bitcast.288, bf16[114,128]{1,0:T(8,128)(2,1)S(1)} %reshape.374, bf16[]{:T(256)} %constant.237, bf16[192,128]{1,0:T(8,128)(2,1)S(1)} %reshape.373, bf16[114,128]{1,0:T(8,128)(2,1)S(1)} %reshape.372, bf16[]{:T(256)} %constant.165.clone.1), kind=kCustom, calls=%fused_computation.261 | custom fusion | flops 322560 | bytes 307460 | tf_op jit(solution)/shard_map/scatter | solution.py:264
  101.1 5.1 %collective-permute-start.8 = (bf16[3,96,128]{2,1,0:T(8,128)(2,1)S(1)}, bf16[3,96,128]{2,1,0:T(8,128)(2,1)S(1)}, u32[]{:S(2)}, u32[]{:S(2)}) collective-permute-start(bf16[3,96,128]{2,1,0:T(8,128)(2,1)S(1)} %get-tuple-element.104), channel_id=1, source_target_pairs={{0,248},{8,0},{16,8},{24,16},{32,24},{40,32},{48,40},{56,48},{64,5... | collective-permute-start | bytes 221192 | tf_op jit(solution)/shard_map/ppermute | solution.py:15
  106.2 2.0 %collective-permute-start.6 = (f32[9088]{0:T(1024)S(1)}, f32[9088]{0:T(1024)S(1)}, u32[]{:S(2)}, u32[]{:S(2)}) collective-permute-start(f32[9088]{0:T(1024)S(1)} %slice_select_fusion.2), channel_id=1, source_target_pairs={{0,4},{2,6},{4,0},{6,2},{1,5},{3,7},{5,1},{7,3},{8,12},{10,14},{12... | collective-permute-start | bytes 109064 | tf_op jit(solution)/shard_map/ppermute | solution.py:53
  108.2 4.5 %collective-permute-done.7 = bf16[3,96,128]{2,1,0:T(8,128)(2,1)S(1)} collective-permute-done((bf16[3,96,128]{2,1,0:T(8,128)(2,1)S(1)}, bf16[3,96,128]{2,1,0:T(8,128)(2,1)S(1)}, u32[]{:S(2)}, u32[]{:S(2)}) %collective-permute-start.7) | collective-permute-done | bytes 73760 | tf_op jit(solution)/shard_map/ppermute | solution.py:15
  112.8 1.5 collective-permute-start.11
  114.3 3.0 %collective-permute-done.11 = bf16[3,96,128]{2,1,0:T(8,128)(2,1)S(1)} collective-permute-done((bf16[3,96,128]{2,1,0:T(8,128)(2,1)S(1)}, bf16[3,96,128]{2,1,0:T(8,128)(2,1)S(1)}, u32[]{:S(2)}, u32[]{:S(2)}) %collective-permute-start.11) | collective-permute-done | bytes 73760 | tf_op jit(solution)/shard_map/ppermute | solution.py:15
  117.5 2.8 %collective-permute-done.9 = f32[9088]{0:T(1024)S(1)} collective-permute-done((f32[9088]{0:T(1024)S(1)}, f32[9088]{0:T(1024)S(1)}, u32[]{:S(2)}, u32[]{:S(2)}) %collective-permute-start.9) | collective-permute-done | bytes 36384 | tf_op jit(solution)/shard_map/ppermute | solution.py:55
  120.3 4.1 %collective-permute-done.10 = f32[9088]{0:T(1024)S(1)} collective-permute-done((f32[9088]{0:T(1024)S(1)}, f32[9088]{0:T(1024)S(1)}, u32[]{:S(2)}, u32[]{:S(2)}) %collective-permute-start.10) | collective-permute-done | bytes 36384 | tf_op jit(solution)/shard_map/ppermute | solution.py:55
  124.7 6.6 %collective-permute-done.13 = f32[9088]{0:T(1024)S(1)} collective-permute-done((f32[9088]{0:T(1024)S(1)}, f32[9088]{0:T(1024)S(1)}, u32[]{:S(2)}, u32[]{:S(2)}) %collective-permute-start.13) | collective-permute-done | bytes 36384 | tf_op jit(solution)/shard_map/ppermute | solution.py:55
  131.4 2.7 %collective-permute-done.14 = f32[9088]{0:T(1024)S(1)} collective-permute-done((f32[9088]{0:T(1024)S(1)}, f32[9088]{0:T(1024)S(1)}, u32[]{:S(2)}, u32[]{:S(2)}) %collective-permute-start.14) | collective-permute-done | bytes 36384 | tf_op jit(solution)/shard_map/ppermute | solution.py:55
  134.3 6.5 %scatter_custom_fusion.2 = f32[1025,128]{1,0:T(8,128)S(1)} fusion(s32[768]{0:T(1024)S(1)} %fusion.132, bf16[768,128]{1,0:T(8,128)(2,1)S(1)} %bitcast.280, f32[]{:T(128)} %constant.184.clone.1), kind=kCustom, calls=%fused_computation.239 | custom fusion | flops 196608 | bytes 721412 | tf_op jit(solution)/shard_map/scatter-add | solution.py:273
  140.8 1.8 %collective-permute-start.16 = (f32[9088]{0:T(1024)S(1)}, f32[9088]{0:T(1024)S(1)}, u32[]{:S(2)}, u32[]{:S(2)}) collective-permute-start(f32[9088]{0:T(1024)S(1)} %add.646), channel_id=1, source_target_pairs={{0,4},{2,6},{4,0},{6,2},{1,5},{3,7},{5,1},{7,3},{8,12},{10,14},{12... | collective-permute-start | bytes 109064 | tf_op jit(solution)/shard_map/ppermute | solution.py:59
  143.4 1.8 %collective-permute-done.16 = f32[9088]{0:T(1024)S(1)} collective-permute-done((f32[9088]{0:T(1024)S(1)}, f32[9088]{0:T(1024)S(1)}, u32[]{:S(2)}, u32[]{:S(2)}) %collective-permute-start.16) | collective-permute-done | bytes 36384 | tf_op jit(solution)/shard_map/ppermute | solution.py:59
  145.2 1.2 collective-permute-start.17
  146.5 2.0 %collective-permute-done.17 = f32[18176]{0:T(1024)S(1)} collective-permute-done((f32[18176]{0:T(1024)S(1)}, f32[18176]{0:T(1024)S(1)}, u32[]{:S(2)}, u32[]{:S(2)}) %collective-permute-start.17) | collective-permute-done | bytes 72736 | tf_op jit(solution)/shard_map/ppermute | solution.py:59
  148.5 9.5 %collective-permute-start.18 = (f32[36352]{0:T(1024)S(1)}, f32[36352]{0:T(1024)S(1)}, u32[]{:S(2)}, u32[]{:S(2)}) collective-permute-start(f32[36352]{0:T(1024)S(1)} %maximum_select_fusion.2), channel_id=1, source_target_pairs={{0,1},{1,0},{2,3},{3,2},{4,5},{5,4},{6,7},{7,6},{8,9},{9,8},{10,11... | collective-permute-start | bytes 436232 | tf_op jit(solution)/shard_map/ppermute | solution.py:59
  (186 shorter events, 21.6 us)
Async XLA Ops:
  0.6 13.2 %copy-start = (bf16[1,1024,128]{2,1,0:T(8,128)(2,1)S(1)}, bf16[1,1024,128]{2,1,0:T(8,128)(2,1)}, u32[]{:S(2)}) copy-start(bf16[1,1024,128]{2,1,0:T(8,128)(2,1)} %param.18) | copy-start | bytes 786436
  0.7 8.1 %copy-start.1 = (s32[1024]{0:T(1024)S(1)}, s32[1024]{0:T(1024)}, u32[]{:S(2)}) copy-start(s32[1024]{0:T(1024)} %param.20) | copy-start | bytes 12292
  17.1 17.3 %copy-start.4 = (s32[1,8,96]{2,1,0:T(8,128)S(1)}, s32[1,8,96]{2,1,0:T(8,128)}, u32[]{:S(2)}) copy-start(s32[1,8,96]{2,1,0:T(8,128)} %param.22) | copy-start | bytes 9220
  17.1 17.3 %copy-start.5 = (bf16[49,128]{1,0:T(8,128)(2,1)S(1)}, bf16[49,128]{1,0:T(8,128)(2,1)}, u32[]{:S(2)}) copy-start(bf16[49,128]{1,0:T(8,128)(2,1)} %param.25) | copy-start | bytes 37636
  17.1 17.4 %copy-start.12 = (s32[1,8]{1,0:T(1,128)S(1)}, s32[1,8]{1,0:T(1,128)}, u32[]{:S(2)}) copy-start(s32[1,8]{1,0:T(1,128)} %param.21) | copy-start | bytes 100
  18.0 33.4 %all-to-all-start = ((bf16[128,9,128]{2,1,0:T(8,128)(2,1)}), bf16[128,9,128]{2,1,0:T(8,128)(2,1)S(1)}, u32[]{:S(2)}, u32[]{:S(2)}) async-start(bf16[128,9,128]{2,1,0:T(8,128)(2,1)} %pad_maximum_fusion), calls=%async_computation | async-start | bytes 1048576 | tf_op jit(solution)/shard_map/all_to_all | solution.py:186
  56.9 6.6 %collective-permute-start.1 = (bf16[3,96,128]{2,1,0:T(8,128)(2,1)S(1)}, bf16[3,96,128]{2,1,0:T(8,128)(2,1)S(1)}, u32[]{:S(2)}, u32[]{:S(2)}) collective-permute-start(bf16[3,96,128]{2,1,0:T(8,128)(2,1)S(1)} %get-tuple-element.108), channel_id=1, source_target_pairs={{0,8},{8,16},{16,24},{24,32},{32,40},{40,48},{48,56},{56,64},{64,7... | collective-permute-start | bytes 221192 | tf_op jit(solution)/shard_map/ppermute | solution.py:15
  57.9 5.6 %collective-permute-start = (bf16[3,96,128]{2,1,0:T(8,128)(2,1)S(1)}, bf16[3,96,128]{2,1,0:T(8,128)(2,1)S(1)}, u32[]{:S(2)}, u32[]{:S(2)}) collective-permute-start(bf16[3,96,128]{2,1,0:T(8,128)(2,1)S(1)} %get-tuple-element.107), channel_id=1, source_target_pairs={{0,248},{8,0},{16,8},{24,16},{32,24},{40,32},{48,40},{56,48},{64,5... | collective-permute-start | bytes 221192 | tf_op jit(solution)/shard_map/ppermute | solution.py:15
  63.5 3.6 %collective-permute-start.2 = (bf16[3,96,128]{2,1,0:T(8,128)(2,1)S(1)}, bf16[3,96,128]{2,1,0:T(8,128)(2,1)S(1)}, u32[]{:S(2)}, u32[]{:S(2)}) collective-permute-start(bf16[3,96,128]{2,1,0:T(8,128)(2,1)S(1)} %pad_maximum_fusion.4), channel_id=1, source_target_pairs={{0,6},{2,0},{4,2},{6,4},{1,7},{3,1},{5,3},{7,5},{8,14},{10,8},{12,... | collective-permute-start | bytes 221192 | tf_op jit(solution)/shard_map/ppermute | solution.py:15
  67.1 4.8 %collective-permute-start.3 = (bf16[3,96,128]{2,1,0:T(8,128)(2,1)S(1)}, bf16[3,96,128]{2,1,0:T(8,128)(2,1)S(1)}, u32[]{:S(2)}, u32[]{:S(2)}) collective-permute-start(bf16[3,96,128]{2,1,0:T(8,128)(2,1)S(1)} %pad_maximum_fusion.5), channel_id=1, source_target_pairs={{0,2},{2,4},{4,6},{6,0},{1,3},{3,5},{5,7},{7,1},{8,10},{10,12},{12... | collective-permute-start | bytes 221192 | tf_op jit(solution)/shard_map/ppermute | solution.py:15
  78.0 0.9 copy-start.7
  78.0 0.9 copy-start.8
  78.0 0.9 copy-start.9
  78.9 1.0 copy-start.2
  78.9 0.9 copy-start.10
  79.0 0.9 copy-start.11
  83.5 1.2 copy-start.13
  86.2 14.7 %collective-permute-start.4 = (f32[36352]{0:T(1024)S(1)}, f32[36352]{0:T(1024)S(1)}, u32[]{:S(2)}, u32[]{:S(2)}) collective-permute-start(f32[36352]{0:T(1024)S(1)} %slice_select_fusion), channel_id=1, source_target_pairs={{0,1},{1,0},{2,3},{3,2},{4,5},{5,4},{6,7},{7,6},{8,9},{9,8},{10,11... | collective-permute-start | bytes 436232 | tf_op jit(solution)/shard_map/ppermute | solution.py:53
  100.9 5.3 %collective-permute-start.5 = (f32[18176]{0:T(1024)S(1)}, f32[18176]{0:T(1024)S(1)}, u32[]{:S(2)}, u32[]{:S(2)}) collective-permute-start(f32[18176]{0:T(1024)S(1)} %slice_select_fusion.1), channel_id=1, source_target_pairs={{0,2},{2,0},{4,6},{6,4},{1,3},{3,1},{5,7},{7,5},{8,10},{10,8},{12,... | collective-permute-start | bytes 218120 | tf_op jit(solution)/shard_map/ppermute | solution.py:53
  101.1 7.2 %collective-permute-start.8 = (bf16[3,96,128]{2,1,0:T(8,128)(2,1)S(1)}, bf16[3,96,128]{2,1,0:T(8,128)(2,1)S(1)}, u32[]{:S(2)}, u32[]{:S(2)}) collective-permute-start(bf16[3,96,128]{2,1,0:T(8,128)(2,1)S(1)} %get-tuple-element.104), channel_id=1, source_target_pairs={{0,248},{8,0},{16,8},{24,16},{32,24},{40,32},{48,40},{56,48},{64,5... | collective-permute-start | bytes 221192 | tf_op jit(solution)/shard_map/ppermute | solution.py:15
  106.2 6.5 %collective-permute-start.7 = (bf16[3,96,128]{2,1,0:T(8,128)(2,1)S(1)}, bf16[3,96,128]{2,1,0:T(8,128)(2,1)S(1)}, u32[]{:S(2)}, u32[]{:S(2)}) collective-permute-start(bf16[3,96,128]{2,1,0:T(8,128)(2,1)S(1)} %get-tuple-element.103), channel_id=1, source_target_pairs={{0,8},{8,16},{16,24},{24,32},{32,40},{40,48},{48,56},{56,64},{64,7... | collective-permute-start | bytes 221192 | tf_op jit(solution)/shard_map/ppermute | solution.py:15
  106.2 6.5 %collective-permute-start.6 = (f32[9088]{0:T(1024)S(1)}, f32[9088]{0:T(1024)S(1)}, u32[]{:S(2)}, u32[]{:S(2)}) collective-permute-start(f32[9088]{0:T(1024)S(1)} %slice_select_fusion.2), channel_id=1, source_target_pairs={{0,4},{2,6},{4,0},{6,2},{1,5},{3,7},{5,1},{7,3},{8,12},{10,14},{12... | collective-permute-start | bytes 109064 | tf_op jit(solution)/shard_map/ppermute | solution.py:53
  112.8 4.5 %collective-permute-start.11 = (bf16[3,96,128]{2,1,0:T(8,128)(2,1)S(1)}, bf16[3,96,128]{2,1,0:T(8,128)(2,1)S(1)}, u32[]{:S(2)}, u32[]{:S(2)}) collective-permute-start(bf16[3,96,128]{2,1,0:T(8,128)(2,1)S(1)} %pad_maximum_fusion.6), channel_id=1, source_target_pairs={{0,2},{2,4},{4,6},{6,0},{1,3},{3,5},{5,7},{7,1},{8,10},{10,12},{12... | collective-permute-start | bytes 221192 | tf_op jit(solution)/shard_map/ppermute | solution.py:15
  117.3 7.1 %collective-permute-start.12 = (bf16[3,96,128]{2,1,0:T(8,128)(2,1)S(1)}, bf16[3,96,128]{2,1,0:T(8,128)(2,1)S(1)}, u32[]{:S(2)}, u32[]{:S(2)}) collective-permute-start(bf16[3,96,128]{2,1,0:T(8,128)(2,1)S(1)} %pad_maximum_fusion.7), channel_id=1, source_target_pairs={{0,6},{2,0},{4,2},{6,4},{1,7},{3,1},{5,3},{7,5},{8,14},{10,8},{12,... | collective-permute-start | bytes 221192 | tf_op jit(solution)/shard_map/ppermute | solution.py:15
  117.4 2.9 %collective-permute-start.9 = (f32[9088]{0:T(1024)S(1)}, f32[9088]{0:T(1024)S(1)}, u32[]{:S(2)}, u32[]{:S(2)}) collective-permute-start(f32[9088]{0:T(1024)S(1)} %select_add_fusion.2), channel_id=1, source_target_pairs={{0,8},{8,0},{16,24},{24,16},{32,40},{40,32},{48,56},{56,48},{64,72... | collective-permute-start | bytes 109064 | tf_op jit(solution)/shard_map/ppermute | solution.py:55
  120.3 4.1 %collective-permute-start.10 = (f32[9088]{0:T(1024)S(1)}, f32[9088]{0:T(1024)S(1)}, u32[]{:S(2)}, u32[]{:S(2)}) collective-permute-start(f32[9088]{0:T(1024)S(1)} %add.641), channel_id=1, source_target_pairs={{0,16},{8,24},{16,0},{24,8},{32,48},{40,56},{48,32},{56,40},{64,80... | collective-permute-start | bytes 109064 | tf_op jit(solution)/shard_map/ppermute | solution.py:55
  124.5 6.8 %collective-permute-start.13 = (f32[9088]{0:T(1024)S(1)}, f32[9088]{0:T(1024)S(1)}, u32[]{:S(2)}, u32[]{:S(2)}) collective-permute-start(f32[9088]{0:T(1024)S(1)} %add.642), channel_id=1, source_target_pairs={{0,32},{8,40},{16,48},{24,56},{32,0},{40,8},{48,16},{56,24},{64,96... | collective-permute-start | bytes 109064 | tf_op jit(solution)/shard_map/ppermute | solution.py:55
  131.3 2.8 %collective-permute-start.14 = (f32[9088]{0:T(1024)S(1)}, f32[9088]{0:T(1024)S(1)}, u32[]{:S(2)}, u32[]{:S(2)}) collective-permute-start(f32[9088]{0:T(1024)S(1)} %add.644), channel_id=1, source_target_pairs={{0,64},{8,72},{16,80},{24,88},{32,96},{40,104},{48,112},{56,120},{... | collective-permute-start | bytes 109064 | tf_op jit(solution)/shard_map/ppermute | solution.py:55
  134.2 6.6 %collective-permute-start.15 = (f32[9088]{0:T(1024)S(1)}, f32[9088]{0:T(1024)S(1)}, u32[]{:S(2)}, u32[]{:S(2)}) collective-permute-start(f32[9088]{0:T(1024)S(1)} %add.645), channel_id=1, source_target_pairs={{0,128},{8,136},{16,144},{24,152},{32,160},{40,168},{48,176},{56,1... | collective-permute-start | bytes 109064 | tf_op jit(solution)/shard_map/ppermute | solution.py:55
  140.8 4.4 %collective-permute-start.16 = (f32[9088]{0:T(1024)S(1)}, f32[9088]{0:T(1024)S(1)}, u32[]{:S(2)}, u32[]{:S(2)}) collective-permute-start(f32[9088]{0:T(1024)S(1)} %add.646), channel_id=1, source_target_pairs={{0,4},{2,6},{4,0},{6,2},{1,5},{3,7},{5,1},{7,3},{8,12},{10,14},{12... | collective-permute-start | bytes 109064 | tf_op jit(solution)/shard_map/ppermute | solution.py:59
  145.2 3.3 %collective-permute-start.17 = (f32[18176]{0:T(1024)S(1)}, f32[18176]{0:T(1024)S(1)}, u32[]{:S(2)}, u32[]{:S(2)}) collective-permute-start(f32[18176]{0:T(1024)S(1)} %maximum_select_fusion.5), channel_id=1, source_target_pairs={{0,2},{2,0},{4,6},{6,4},{1,3},{3,1},{5,7},{7,5},{8,10},{10,8},{12,... | collective-permute-start | bytes 218120 | tf_op jit(solution)/shard_map/ppermute | solution.py:59
  148.5 10.5 %collective-permute-start.18 = (f32[36352]{0:T(1024)S(1)}, f32[36352]{0:T(1024)S(1)}, u32[]{:S(2)}, u32[]{:S(2)}) collective-permute-start(f32[36352]{0:T(1024)S(1)} %maximum_select_fusion.2), channel_id=1, source_target_pairs={{0,1},{1,0},{2,3},{3,2},{4,5},{5,4},{6,7},{7,6},{8,9},{9,8},{10,11... | collective-permute-start | bytes 436232 | tf_op jit(solution)/shard_map/ppermute | solution.py:59
  (2 other events, 1.6 us)

commit v2 on v1

--- a/solution.py
+++ b/solution.py
@@ -43,21 +43,38 @@
     total = flat.shape[0]
     pad = (-total) % (1 << len(halving))
     buf = jnp.pad(flat, (0, pad))
-    for axis, bit, size in halving:
-        upper = (lax.axis_index(axis) // bit) % 2 == 1
-        half = buf.shape[0] // 2
-        low, high = buf[:half], buf[half:]
-        keep = jnp.where(upper, high, low)
-        send = jnp.where(upper, low, high)
-        pairs = [(i, i ^ bit) for i in range(size)]
-        buf = stepped(keep + lax.ppermute(send, axis, pairs))
+    for axis in halving_axes:
+        size = lax.axis_size(axis)
+        digit = lax.axis_index(axis)
+        chunks = jnp.split(buf, size)
+
+        def chunk_at(index):
+            chosen = chunks[size - 1]
+            for place in reversed(range(size - 1)):
+                chosen = jnp.where(index == place, chunks[place], chosen)
+            return chosen
+
+        total_chunk = chunk_at(digit)
+        for flip in range(1, size):
+            pairs = [(i, i ^ flip) for i in range(size)]
+            total_chunk = total_chunk + lax.ppermute(chunk_at(digit ^ flip), axis, pairs)
+        buf = stepped(total_chunk)
     for axis, bit, size in bits_of(doubling_axes):
         buf = stepped(buf + lax.ppermute(buf, axis, [(i, i ^ bit) for i in range(size)]))
-    for axis, bit, size in reversed(halving):
-        upper = (lax.axis_index(axis) // bit) % 2 == 1
-        pairs = [(i, i ^ bit) for i in range(size)]
-        got = lax.ppermute(buf, axis, pairs)
-        buf = stepped(jnp.where(upper, jnp.concatenate([got, buf]), jnp.concatenate([buf, got])))
+    for axis in reversed(halving_axes):
+        size = lax.axis_size(axis)
+        digit = lax.axis_index(axis)
+        pieces = [buf] + [
+            lax.ppermute(buf, axis, [(i, i ^ flip) for i in range(size)]) for flip in range(1, size)
+        ]
+        placed = []
+        for place in range(size):
+            source = place ^ digit
+            chosen = pieces[size - 1]
+            for flip in reversed(range(size - 1)):
+                chosen = jnp.where(source == flip, pieces[flip], chosen)
+            placed.append(chosen)
+        buf = stepped(jnp.concatenate(placed))
     out = []
     start = 0
     for part in parts:

time: 162 us -> 162 us (level)
  starting transfers between devices: 52.2 us -> 48 us
  waiting for transfers between devices: 52.6 us -> 55.9 us
    ppermute x8, starting transfers between devices: 14.4 us -> 8.45 us  [from_behind(): return lax.ppermute(value, axis, pairs)]
    ppermute x6 -> x8, waiting for transfers between devices: 4.77 us -> 0.24 us  [the longest x4 0.23 us: tree_sum(): lax.ppermute(buf, axis, [(i, i ^ flip) for i in range(size)])]
    ppermute x5, waiting for transfers between devices: 16.2 us -> 20.4 us  [tree_sum(): lax.ppermute(buf, axis, [(i, i ^ bit) for i in range(size)])]
    ppermute x8, waiting for transfers between devices: 14.7 us -> 18.4 us  [from_behind(): return lax.ppermute(value, axis, pairs)]
    ppermute x6 -> x8, starting transfers between devices: 21.3 us -> 22.9 us  [the longest x4 12.6 us: tree_sum(): lax.ppermute(buf, axis, [(i, i ^ flip) for i in range(size)])]
  transfers between devices with their start and end apart: 20 -> 22, of which waited for: 13 -> 12; matrix products, arithmetic and copies ran while one was open for 10% -> 10% of each run, Pallas kernels for 0% -> 0%
where the time goes in v2:
time: 162 us
  waiting for transfers between devices  55.9 us (35%)
  starting transfers between devices  48 us (30%)
  other arithmetic  33.1 us (20%)
  local copies, waits for them, and re-layouts  19.9 us (12%)
  matrix products  3.2 us (2%)
    ppermute x5, waiting for transfers between devices, tree_sum(): lax.ppermute(buf, axis, [(i, i ^ bit) for i in range(size)])  20.4 us
    ppermute x8, waiting for transfers between devices, from_behind(): return lax.ppermute(value, axis, pairs)  18.4 us
    all_to_all x1, waiting for transfers between devices, local(): lax.all_to_all(jnp.concatenate([outgoing, label_row], axis=1), ('face', '...  16.8 us
    all_to_all x1, starting transfers between devices, local(): lax.all_to_all(jnp.concatenate([outgoing, label_row], axis=1), ('face', '...  16.3 us
    ppermute x4, starting transfers between devices, tree_sum(): lax.ppermute(buf, axis, [(i, i ^ flip) for i in range(size)])  12.6 us
    ppermute x4, starting transfers between devices, tree_sum(): lax.ppermute(chunk_at(digit ^ flip), axis, pairs)  10.3 us
    ppermute x8, starting transfers between devices, from_behind(): return lax.ppermute(value, axis, pairs)  8.45 us
    scatter-add x1, other arithmetic, finish(): incoming = jnp.zeros((pixel_count + 1, channels), jnp.float32).at[send_pi...  6.52 us
  transfers between devices with their start and end apart: 22, of which 12 were waited for; matrix products, arithmetic and copies ran while one was open for 10% of the time, Pallas kernels for 0%

profile of v2, /device:TPU:1, one launch (start us, length us, event | category | flops | bytes accessed | tf_op | source)
XLA Modules:
  0.0 161.7 jit_solution(8703727099525557560)
XLA Ops:
  3.7 5.1 %sort.17 = (s32[1024]{0:T(1024)}, s32[1024]{0:T(1024)S(1)}) sort(s32[1024]{0:T(1024)} %param.19, s32[1024]{0:T(1024)S(1)} %iota.8), dimensions={0}, to_apply=%region_0.0 | sort | flops 10240 | bytes 16384 | tf_op jit(solution)/shard_map/jit(argsort)/sort | solution.py:198
  8.8 4.5 %gather_fusion.1 = s32[1024]{0:T(1024)S(1)} fusion(s32[1024]{0:T(1024)S(1)} %copy-done.1, s32[1024]{0:T(1024)S(1)} %get-tuple-element.183), kind=kCustom, calls=%fused_computation.1 | custom fusion | bytes 12288 | tf_op jit(solution)/shard_map/gather | solution.py:200
  13.8 3.2 %gather_fusion = bf16[1024,128]{1,0:T(8,128)(2,1)S(1)} fusion(bf16[1024,128]{1,0:T(8,128)(2,1)S(1)} %bitcast.274, s32[1024]{0:T(1024)S(1)} %get-tuple-element.183), kind=kCustom, calls=%fused_computation | custom fusion | bytes 528384 | tf_op jit(solution)/shard_map/gather | solution.py:199
  17.1 0.9 pad_maximum_fusion
  18.0 16.3 %all-to-all-start = ((bf16[128,9,128]{2,1,0:T(8,128)(2,1)}), bf16[128,9,128]{2,1,0:T(8,128)(2,1)S(1)}, u32[]{:S(2)}, u32[]{:S(2)}) async-start(bf16[128,9,128]{2,1,0:T(8,128)(2,1)} %pad_maximum_fusion), calls=%async_computation | async-start | bytes 1048576 | tf_op jit(solution)/shard_map/all_to_all | solution.py:203
  34.5 16.8 %all-to-all-done = bf16[128,9,128]{2,1,0:T(8,128)(2,1)S(1)} async-done(((bf16[128,9,128]{2,1,0:T(8,128)(2,1)}), bf16[128,9,128]{2,1,0:T(8,128)(2,1)S(1)}, u32[]{:S(2)}, u32[]{:S(2)}) %all-to-all-start) | async-done | bytes 294944 | tf_op jit(solution)/shard_map/all_to_all | solution.py:203
  51.6 3.2 %scatter_custom_fusion = bf16[1024,128]{1,0:T(8,128)(2,1)S(1)} fusion(s32[1024]{0:T(1024)S(1)} %bitcast.289, bf16[128,9,128]{2,1,0:T(8,128)(2,1)S(1)} %all-to-all-done, bf16[]{:T(256)} %constant.58.clone.1), kind=kCustom, calls=%fused_computation.246 | custom fusion | bytes 524290 | tf_op jit(solution)/shard_map/scatter | solution.py:216
  54.9 1.9 %gather_fusion.2 = bf16[768,128]{1,0:T(8,128)(2,1)S(1)} fusion(bf16[1025,128]{1,0:T(8,128)(2,1)S(1)} %concatenate.47, s32[1024]{0:T(1024)S(1)} %pad_clamp_fusion.1), kind=kCustom, calls=%fused_computation.2 | custom fusion | bytes 396288 | tf_op jit(solution)/shard_map/gather | solution.py:230
  56.9 2.8 %collective-permute-start = (bf16[3,96,128]{2,1,0:T(8,128)(2,1)S(1)}, bf16[3,96,128]{2,1,0:T(8,128)(2,1)S(1)}, u32[]{:S(2)}, u32[]{:S(2)}) collective-permute-start(bf16[3,96,128]{2,1,0:T(8,128)(2,1)S(1)} %get-tuple-element.104), channel_id=1, source_target_pairs={{0,248},{8,0},{16,8},{24,16},{32,24},{40,32},{48,40},{56,48},{64,5... | collective-permute-start | bytes 221192 | tf_op jit(solution)/shard_map/ppermute | solution.py:15
  59.7 1.4 collective-permute-done
  61.1 5.1 %collective-permute-done.1 = bf16[3,96,128]{2,1,0:T(8,128)(2,1)S(1)} collective-permute-done((bf16[3,96,128]{2,1,0:T(8,128)(2,1)S(1)}, bf16[3,96,128]{2,1,0:T(8,128)(2,1)S(1)}, u32[]{:S(2)}, u32[]{:S(2)}) %collective-permute-start.1) | collective-permute-done | bytes 73760 | tf_op jit(solution)/shard_map/ppermute | solution.py:15
  66.3 3.3 %collective-permute-done.2 = bf16[3,96,128]{2,1,0:T(8,128)(2,1)S(1)} collective-permute-done((bf16[3,96,128]{2,1,0:T(8,128)(2,1)S(1)}, bf16[3,96,128]{2,1,0:T(8,128)(2,1)S(1)}, u32[]{:S(2)}, u32[]{:S(2)}) %collective-permute-start.2) | collective-permute-done | bytes 73760 | tf_op jit(solution)/shard_map/ppermute | solution.py:15
  70.2 4.1 %collective-permute-done.3 = bf16[3,96,128]{2,1,0:T(8,128)(2,1)S(1)} collective-permute-done((bf16[3,96,128]{2,1,0:T(8,128)(2,1)S(1)}, bf16[3,96,128]{2,1,0:T(8,128)(2,1)S(1)}, u32[]{:S(2)}, u32[]{:S(2)}) %collective-permute-start.3) | collective-permute-done | bytes 73760 | tf_op jit(solution)/shard_map/ppermute | solution.py:15
  74.5 1.5 gather_fusion.3
  76.6 3.8 %add_reduce_fusion = (f32[32,32]{1,0:T(8,128)S(1)}, f32[32,32,128]{2,1,0:T(8,128)S(1)}) fusion(f32[128]{0:T(128)S(1)} %copy-done.6, f32[128]{0:T(128)S(1)} %get-tuple-element.130, f32[38,38,128]{2,1,0:T(8,128)S(1)} %maximum_convert_fusion, f32[128]{0:T(128)S(1)} %get-tuple-element.131, f32[128]{0:T(128)S(1)} %get-tuple-element.132, ...), kind=kLoop, calls=%fused_computation.237 | loop fusion | flops 12975104 | bytes 26244096 | tf_op jit(solution)/shard_map/reduce_sum | solution.py:240
  85.1 0.9 multiply_reduce_fusion.1
  85.9 0.9 multiply_reduce_fusion.19
  87.1 1.0 fusion.107
  88.6 6.3 %collective-permute-start.4 = (f32[36352]{0:T(1024)S(1)}, f32[36352]{0:T(1024)S(1)}, u32[]{:S(2)}, u32[]{:S(2)}) collective-permute-start(f32[36352]{0:T(1024)S(1)} %slice_select_fusion), channel_id=1, source_target_pairs={{0,1},{1,0},{2,3},{3,2},{4,5},{5,4},{6,7},{7,6},{8,9},{9,8},{10,11... | collective-permute-start | bytes 436232 | tf_op jit(solution)/shard_map/ppermute | solution.py:60
  94.9 6.1 %fusion.137 = (bf16[38,38,128]{2,1,0:T(8,128)(2,1)S(1)}, f32[38,38,128]{2,1,0:T(8,128)S(1)}) fusion(f32[128]{0:T(128)S(1)} %get-tuple-element.129, f32[128]{0:T(128)S(1)} %get-tuple-element.148, f32[128]{0:T(128)S(1)} %get-tuple-element.167, f32[128]{0:T(128)S(1)} %get-tuple-element.177, f32[128]{0:T(128)S(1)} %get-tuple-element.176, ...), kind=kLoop, calls=%fused_computation.402 | loop fusion | flops 18113536 | bytes 1658368 | tf_op jit(solution)/shard_map/convert.15
  101.2 1.6 %scatter_custom_fusion.1 = bf16[769,128]{1,0:T(8,128)(2,1)S(1)} fusion(s32[420]{0:T(512)S(1)} %bitcast.286, bf16[114,128]{1,0:T(8,128)(2,1)S(1)} %reshape.362, bf16[]{:T(256)} %constant.170, bf16[192,128]{1,0:T(8,128)(2,1)S(1)} %reshape.361, bf16[114,128]{1,0:T(8,128)(2,1)S(1)} %reshape.360, bf16[]{:T(256)} %constant.58.clone.1), kind=kCustom, calls=%fused_computation.256 | custom fusion | flops 322560 | bytes 307460 | tf_op jit(solution)/shard_map/scatter | solution.py:281
  103.4 3.6 %collective-permute-start.6 = (f32[9088]{0:T(1024)S(1)}, f32[9088]{0:T(1024)S(1)}, u32[]{:S(2)}, u32[]{:S(2)}) collective-permute-start(f32[9088]{0:T(1024)S(1)} %get-tuple-element.116), channel_id=1, source_target_pairs={{0,4},{2,6},{4,0},{6,2},{1,5},{3,7},{5,1},{7,3},{8,12},{10,14},{12... | collective-permute-start | bytes 109064 | tf_op jit(solution)/shard_map/ppermute | solution.py:60
  107.1 4.8 %collective-permute-start.10 = (bf16[3,96,128]{2,1,0:T(8,128)(2,1)S(1)}, bf16[3,96,128]{2,1,0:T(8,128)(2,1)S(1)}, u32[]{:S(2)}, u32[]{:S(2)}) collective-permute-start(bf16[3,96,128]{2,1,0:T(8,128)(2,1)S(1)} %get-tuple-element.101), channel_id=1, source_target_pairs={{0,248},{8,0},{16,8},{24,16},{32,24},{40,32},{48,40},{56,48},{64,5... | collective-permute-start | bytes 221192 | tf_op jit(solution)/shard_map/ppermute | solution.py:15
  112.1 3.1 %collective-permute-done.8 = f32[9088]{0:T(1024)S(1)} collective-permute-done((f32[9088]{0:T(1024)S(1)}, f32[9088]{0:T(1024)S(1)}, u32[]{:S(2)}, u32[]{:S(2)}) %collective-permute-start.8) | collective-permute-done | bytes 36384 | tf_op jit(solution)/shard_map/ppermute | solution.py:63
  115.3 4.4 %collective-permute-done.13 = bf16[3,96,128]{2,1,0:T(8,128)(2,1)S(1)} collective-permute-done((bf16[3,96,128]{2,1,0:T(8,128)(2,1)S(1)}, bf16[3,96,128]{2,1,0:T(8,128)(2,1)S(1)}, u32[]{:S(2)}, u32[]{:S(2)}) %collective-permute-start.13) | collective-permute-done | bytes 73760 | tf_op jit(solution)/shard_map/ppermute | solution.py:15
  120.0 3.7 %collective-permute-done.11 = f32[9088]{0:T(1024)S(1)} collective-permute-done((f32[9088]{0:T(1024)S(1)}, f32[9088]{0:T(1024)S(1)}, u32[]{:S(2)}, u32[]{:S(2)}) %collective-permute-start.11) | collective-permute-done | bytes 36384 | tf_op jit(solution)/shard_map/ppermute | solution.py:63
  123.7 6.7 %collective-permute-done.12 = f32[9088]{0:T(1024)S(1)} collective-permute-done((f32[9088]{0:T(1024)S(1)}, f32[9088]{0:T(1024)S(1)}, u32[]{:S(2)}, u32[]{:S(2)}) %collective-permute-start.12) | collective-permute-done | bytes 36384 | tf_op jit(solution)/shard_map/ppermute | solution.py:63
  130.6 2.7 %collective-permute-done.15 = f32[9088]{0:T(1024)S(1)} collective-permute-done((f32[9088]{0:T(1024)S(1)}, f32[9088]{0:T(1024)S(1)}, u32[]{:S(2)}, u32[]{:S(2)}) %collective-permute-start.15) | collective-permute-done | bytes 36384 | tf_op jit(solution)/shard_map/ppermute | solution.py:63
  133.5 4.2 %collective-permute-done.16 = f32[9088]{0:T(1024)S(1)} collective-permute-done((f32[9088]{0:T(1024)S(1)}, f32[9088]{0:T(1024)S(1)}, u32[]{:S(2)}, u32[]{:S(2)}) %collective-permute-start.16) | collective-permute-done | bytes 36384 | tf_op jit(solution)/shard_map/ppermute | solution.py:63
  137.7 3.4 %collective-permute-start.18 = (f32[9088]{0:T(1024)S(1)}, f32[9088]{0:T(1024)S(1)}, u32[]{:S(2)}, u32[]{:S(2)}) collective-permute-start(f32[9088]{0:T(1024)S(1)} %add.631), channel_id=1, source_target_pairs={{0,4},{2,6},{4,0},{6,2},{1,5},{3,7},{5,1},{7,3},{8,12},{10,14},{12... | collective-permute-start | bytes 109064 | tf_op jit(solution)/shard_map/ppermute | solution.py:68
  141.2 6.5 %scatter_custom_fusion.2 = f32[1025,128]{1,0:T(8,128)S(1)} fusion(s32[768]{0:T(1024)S(1)} %fusion.131, bf16[768,128]{1,0:T(8,128)(2,1)S(1)} %bitcast.281, f32[]{:T(128)} %constant.131.clone.1), kind=kCustom, calls=%fused_computation.239 | custom fusion | flops 196608 | bytes 721412 | tf_op jit(solution)/shard_map/scatter-add | solution.py:290
  147.8 9.2 %collective-permute-start.20 = (f32[36352]{0:T(1024)S(1)}, f32[36352]{0:T(1024)S(1)}, u32[]{:S(2)}, u32[]{:S(2)}) collective-permute-start(f32[36352]{0:T(1024)S(1)} %pad_maximum_fusion.2), channel_id=1, source_target_pairs={{0,1},{1,0},{2,3},{3,2},{4,5},{5,4},{6,7},{7,6},{8,9},{9,8},{10,11... | collective-permute-start | bytes 436232 | tf_op jit(solution)/shard_map/ppermute | solution.py:68
  (185 shorter events, 17.0 us)
Async XLA Ops:
  0.6 13.2 %copy-start = (bf16[1,1024,128]{2,1,0:T(8,128)(2,1)S(1)}, bf16[1,1024,128]{2,1,0:T(8,128)(2,1)}, u32[]{:S(2)}) copy-start(bf16[1,1024,128]{2,1,0:T(8,128)(2,1)} %param.18) | copy-start | bytes 786436
  0.7 8.1 %copy-start.1 = (s32[1024]{0:T(1024)S(1)}, s32[1024]{0:T(1024)}, u32[]{:S(2)}) copy-start(s32[1024]{0:T(1024)} %param.20) | copy-start | bytes 12292
  17.1 17.3 %copy-start.4 = (s32[1,8,96]{2,1,0:T(8,128)S(1)}, s32[1,8,96]{2,1,0:T(8,128)}, u32[]{:S(2)}) copy-start(s32[1,8,96]{2,1,0:T(8,128)} %param.22) | copy-start | bytes 9220
  17.1 17.4 %copy-start.5 = (bf16[49,128]{1,0:T(8,128)(2,1)S(1)}, bf16[49,128]{1,0:T(8,128)(2,1)}, u32[]{:S(2)}) copy-start(bf16[49,128]{1,0:T(8,128)(2,1)} %param.25) | copy-start | bytes 37636
  17.1 17.4 %copy-start.12 = (s32[1,8]{1,0:T(1,128)S(1)}, s32[1,8]{1,0:T(1,128)}, u32[]{:S(2)}) copy-start(s32[1,8]{1,0:T(1,128)} %param.21) | copy-start | bytes 100
  18.0 33.4 %all-to-all-start = ((bf16[128,9,128]{2,1,0:T(8,128)(2,1)}), bf16[128,9,128]{2,1,0:T(8,128)(2,1)S(1)}, u32[]{:S(2)}, u32[]{:S(2)}) async-start(bf16[128,9,128]{2,1,0:T(8,128)(2,1)} %pad_maximum_fusion), calls=%async_computation | async-start | bytes 1048576 | tf_op jit(solution)/shard_map/all_to_all | solution.py:203
  56.9 4.2 %collective-permute-start = (bf16[3,96,128]{2,1,0:T(8,128)(2,1)S(1)}, bf16[3,96,128]{2,1,0:T(8,128)(2,1)S(1)}, u32[]{:S(2)}, u32[]{:S(2)}) collective-permute-start(bf16[3,96,128]{2,1,0:T(8,128)(2,1)S(1)} %get-tuple-element.104), channel_id=1, source_target_pairs={{0,248},{8,0},{16,8},{24,16},{32,24},{40,32},{48,40},{56,48},{64,5... | collective-permute-start | bytes 221192 | tf_op jit(solution)/shard_map/ppermute | solution.py:15
  59.7 6.5 %collective-permute-start.1 = (bf16[3,96,128]{2,1,0:T(8,128)(2,1)S(1)}, bf16[3,96,128]{2,1,0:T(8,128)(2,1)S(1)}, u32[]{:S(2)}, u32[]{:S(2)}) collective-permute-start(bf16[3,96,128]{2,1,0:T(8,128)(2,1)S(1)} %get-tuple-element.105), channel_id=1, source_target_pairs={{0,8},{8,16},{16,24},{24,32},{32,40},{40,48},{48,56},{56,64},{64,7... | collective-permute-start | bytes 221192 | tf_op jit(solution)/shard_map/ppermute | solution.py:15
  66.2 3.4 %collective-permute-start.2 = (bf16[3,96,128]{2,1,0:T(8,128)(2,1)S(1)}, bf16[3,96,128]{2,1,0:T(8,128)(2,1)S(1)}, u32[]{:S(2)}, u32[]{:S(2)}) collective-permute-start(bf16[3,96,128]{2,1,0:T(8,128)(2,1)S(1)} %pad_maximum_fusion.4), channel_id=1, source_target_pairs={{0,6},{2,0},{4,2},{6,4},{1,7},{3,1},{5,3},{7,5},{8,14},{10,8},{12,... | collective-permute-start | bytes 221192 | tf_op jit(solution)/shard_map/ppermute | solution.py:15
  69.7 4.7 %collective-permute-start.3 = (bf16[3,96,128]{2,1,0:T(8,128)(2,1)S(1)}, bf16[3,96,128]{2,1,0:T(8,128)(2,1)S(1)}, u32[]{:S(2)}, u32[]{:S(2)}) collective-permute-start(bf16[3,96,128]{2,1,0:T(8,128)(2,1)S(1)} %pad_maximum_fusion.5), channel_id=1, source_target_pairs={{0,2},{2,4},{4,6},{6,0},{1,3},{3,5},{5,7},{7,1},{8,10},{10,12},{12... | collective-permute-start | bytes 221192 | tf_op jit(solution)/shard_map/ppermute | solution.py:15
  80.4 0.9 copy-start.8
  80.4 0.9 copy-start.9
  81.3 1.0 copy-start.2
  81.3 0.9 copy-start.10
  85.9 1.2 copy-start.13
  88.6 14.3 %collective-permute-start.4 = (f32[36352]{0:T(1024)S(1)}, f32[36352]{0:T(1024)S(1)}, u32[]{:S(2)}, u32[]{:S(2)}) collective-permute-start(f32[36352]{0:T(1024)S(1)} %slice_select_fusion), channel_id=1, source_target_pairs={{0,1},{1,0},{2,3},{3,2},{4,5},{5,4},{6,7},{7,6},{8,9},{9,8},{10,11... | collective-permute-start | bytes 436232 | tf_op jit(solution)/shard_map/ppermute | solution.py:60
  103.0 8.9 %collective-permute-start.7 = (f32[9088]{0:T(1024)S(1)}, f32[9088]{0:T(1024)S(1)}, u32[]{:S(2)}, u32[]{:S(2)}) collective-permute-start(f32[9088]{0:T(1024)S(1)} %select_select_fusion.4), channel_id=1, source_target_pairs={{0,6},{2,4},{4,2},{6,0},{1,7},{3,5},{5,3},{7,1},{8,14},{10,12},{12... | collective-permute-start | bytes 109064 | tf_op jit(solution)/shard_map/ppermute | solution.py:60
  103.3 8.6 %collective-permute-start.5 = (f32[9088]{0:T(1024)S(1)}, f32[9088]{0:T(1024)S(1)}, u32[]{:S(2)}, u32[]{:S(2)}) collective-permute-start(f32[9088]{0:T(1024)S(1)} %get-tuple-element.115), channel_id=1, source_target_pairs={{0,2},{2,0},{4,6},{6,4},{1,3},{3,1},{5,7},{7,5},{8,10},{10,8},{12,... | collective-permute-start | bytes 109064 | tf_op jit(solution)/shard_map/ppermute | solution.py:60
  103.4 8.5 %collective-permute-start.6 = (f32[9088]{0:T(1024)S(1)}, f32[9088]{0:T(1024)S(1)}, u32[]{:S(2)}, u32[]{:S(2)}) collective-permute-start(f32[9088]{0:T(1024)S(1)} %get-tuple-element.116), channel_id=1, source_target_pairs={{0,4},{2,6},{4,0},{6,2},{1,5},{3,7},{5,1},{7,3},{8,12},{10,14},{12... | collective-permute-start | bytes 109064 | tf_op jit(solution)/shard_map/ppermute | solution.py:60
  107.0 8.1 %collective-permute-start.9 = (bf16[3,96,128]{2,1,0:T(8,128)(2,1)S(1)}, bf16[3,96,128]{2,1,0:T(8,128)(2,1)S(1)}, u32[]{:S(2)}, u32[]{:S(2)}) collective-permute-start(bf16[3,96,128]{2,1,0:T(8,128)(2,1)S(1)} %get-tuple-element.100), channel_id=1, source_target_pairs={{0,8},{8,16},{16,24},{24,32},{32,40},{40,48},{48,56},{56,64},{64,7... | collective-permute-start | bytes 221192 | tf_op jit(solution)/shard_map/ppermute | solution.py:15
  107.1 8.0 %collective-permute-start.10 = (bf16[3,96,128]{2,1,0:T(8,128)(2,1)S(1)}, bf16[3,96,128]{2,1,0:T(8,128)(2,1)S(1)}, u32[]{:S(2)}, u32[]{:S(2)}) collective-permute-start(bf16[3,96,128]{2,1,0:T(8,128)(2,1)S(1)} %get-tuple-element.101), channel_id=1, source_target_pairs={{0,248},{8,0},{16,8},{24,16},{32,24},{40,32},{48,40},{56,48},{64,5... | collective-permute-start | bytes 221192 | tf_op jit(solution)/shard_map/ppermute | solution.py:15
  111.9 3.2 %collective-permute-start.8 = (f32[9088]{0:T(1024)S(1)}, f32[9088]{0:T(1024)S(1)}, u32[]{:S(2)}, u32[]{:S(2)}) collective-permute-start(f32[9088]{0:T(1024)S(1)} %add_add_fusion), channel_id=1, source_target_pairs={{0,8},{8,0},{16,24},{24,16},{32,40},{40,32},{48,56},{56,48},{64,72... | collective-permute-start | bytes 109064 | tf_op jit(solution)/shard_map/ppermute | solution.py:63
  115.2 4.5 %collective-permute-start.13 = (bf16[3,96,128]{2,1,0:T(8,128)(2,1)S(1)}, bf16[3,96,128]{2,1,0:T(8,128)(2,1)S(1)}, u32[]{:S(2)}, u32[]{:S(2)}) collective-permute-start(bf16[3,96,128]{2,1,0:T(8,128)(2,1)S(1)} %pad_maximum_fusion.6), channel_id=1, source_target_pairs={{0,2},{2,4},{4,6},{6,0},{1,3},{3,5},{5,7},{7,1},{8,10},{10,12},{12... | collective-permute-start | bytes 221192 | tf_op jit(solution)/shard_map/ppermute | solution.py:15
  119.8 10.6 %collective-permute-start.14 = (bf16[3,96,128]{2,1,0:T(8,128)(2,1)S(1)}, bf16[3,96,128]{2,1,0:T(8,128)(2,1)S(1)}, u32[]{:S(2)}, u32[]{:S(2)}) collective-permute-start(bf16[3,96,128]{2,1,0:T(8,128)(2,1)S(1)} %pad_maximum_fusion.7), channel_id=1, source_target_pairs={{0,6},{2,0},{4,2},{6,4},{1,7},{3,1},{5,3},{7,5},{8,14},{10,8},{12,... | collective-permute-start | bytes 221192 | tf_op jit(solution)/shard_map/ppermute | solution.py:15
  119.9 3.8 %collective-permute-start.11 = (f32[9088]{0:T(1024)S(1)}, f32[9088]{0:T(1024)S(1)}, u32[]{:S(2)}, u32[]{:S(2)}) collective-permute-start(f32[9088]{0:T(1024)S(1)} %add.626), channel_id=1, source_target_pairs={{0,16},{8,24},{16,0},{24,8},{32,48},{40,56},{48,32},{56,40},{64,80... | collective-permute-start | bytes 109064 | tf_op jit(solution)/shard_map/ppermute | solution.py:63
  123.7 6.7 %collective-permute-start.12 = (f32[9088]{0:T(1024)S(1)}, f32[9088]{0:T(1024)S(1)}, u32[]{:S(2)}, u32[]{:S(2)}) collective-permute-start(f32[9088]{0:T(1024)S(1)} %add.627), channel_id=1, source_target_pairs={{0,32},{8,40},{16,48},{24,56},{32,0},{40,8},{48,16},{56,24},{64,96... | collective-permute-start | bytes 109064 | tf_op jit(solution)/shard_map/ppermute | solution.py:63
  130.5 2.9 %collective-permute-start.15 = (f32[9088]{0:T(1024)S(1)}, f32[9088]{0:T(1024)S(1)}, u32[]{:S(2)}, u32[]{:S(2)}) collective-permute-start(f32[9088]{0:T(1024)S(1)} %add.628), channel_id=1, source_target_pairs={{0,64},{8,72},{16,80},{24,88},{32,96},{40,104},{48,112},{56,120},{... | collective-permute-start | bytes 109064 | tf_op jit(solution)/shard_map/ppermute | solution.py:63
  133.4 4.3 %collective-permute-start.16 = (f32[9088]{0:T(1024)S(1)}, f32[9088]{0:T(1024)S(1)}, u32[]{:S(2)}, u32[]{:S(2)}) collective-permute-start(f32[9088]{0:T(1024)S(1)} %add.630), channel_id=1, source_target_pairs={{0,128},{8,136},{16,144},{24,152},{32,160},{40,168},{48,176},{56,1... | collective-permute-start | bytes 109064 | tf_op jit(solution)/shard_map/ppermute | solution.py:63
  137.7 10.0 %collective-permute-start.19 = (f32[9088]{0:T(1024)S(1)}, f32[9088]{0:T(1024)S(1)}, u32[]{:S(2)}, u32[]{:S(2)}) collective-permute-start(f32[9088]{0:T(1024)S(1)} %add.631), channel_id=1, source_target_pairs={{0,6},{2,4},{4,2},{6,0},{1,7},{3,5},{5,3},{7,1},{8,14},{10,12},{12... | collective-permute-start | bytes 109064 | tf_op jit(solution)/shard_map/ppermute | solution.py:68
  137.7 10.0 %collective-permute-start.18 = (f32[9088]{0:T(1024)S(1)}, f32[9088]{0:T(1024)S(1)}, u32[]{:S(2)}, u32[]{:S(2)}) collective-permute-start(f32[9088]{0:T(1024)S(1)} %add.631), channel_id=1, source_target_pairs={{0,4},{2,6},{4,0},{6,2},{1,5},{3,7},{5,1},{7,3},{8,12},{10,14},{12... | collective-permute-start | bytes 109064 | tf_op jit(solution)/shard_map/ppermute | solution.py:68
  141.1 6.6 %collective-permute-start.17 = (f32[9088]{0:T(1024)S(1)}, f32[9088]{0:T(1024)S(1)}, u32[]{:S(2)}, u32[]{:S(2)}) collective-permute-start(f32[9088]{0:T(1024)S(1)} %add.631), channel_id=1, source_target_pairs={{0,2},{2,0},{4,6},{6,4},{1,3},{3,1},{5,7},{7,5},{8,10},{10,8},{12,... | collective-permute-start | bytes 109064 | tf_op jit(solution)/shard_map/ppermute | solution.py:68
  147.8 10.2 %collective-permute-start.20 = (f32[36352]{0:T(1024)S(1)}, f32[36352]{0:T(1024)S(1)}, u32[]{:S(2)}, u32[]{:S(2)}) collective-permute-start(f32[36352]{0:T(1024)S(1)} %pad_maximum_fusion.2), channel_id=1, source_target_pairs={{0,1},{1,0},{2,3},{3,2},{4,5},{5,4},{6,7},{7,6},{8,9},{9,8},{10,11... | collective-permute-start | bytes 436232 | tf_op jit(solution)/shard_map/ppermute | solution.py:68
  (4 other events, 3.4 us)

commit v3 on v2

--- a/solution.py
+++ b/solution.py
@@ -195,9 +195,11 @@
     tile_side = math.isqrt(pixel_count)
     cycle_rows, cycle_cols = cycle_cells(tile_side)
     factor = 1.0 / math.sqrt(lax.axis_size("dp") * tile_count * pixel_count)
-    ordering = jnp.argsort(row_tile, stable=True)
+    _, ordering, sorted_pixels = lax.sort(
+        (row_tile, jnp.arange(row_tile.shape[0], dtype=jnp.int32), row_pixel), num_keys=1, is_stable=True
+    )
     outgoing = loader[0][ordering].reshape(tile_count, per_peer, channels)
-    labels = row_pixel[ordering].reshape(tile_count, per_peer)
+    labels = sorted_pixels.reshape(tile_count, per_peer)
     digits = jnp.concatenate([labels // 32, labels % 32], axis=1).astype(loader.dtype)
     label_row = jnp.pad(digits, ((0, 0), (0, channels - 2 * per_peer)))[:, None, :]
     parcel = lax.all_to_all(

time: 162 us -> 158 us (0.975)
  local copies, waits for them, and re-layouts: 19.9 us -> 15.4 us
    gather x1 -> x0, local copies, waits for them, and re-layouts: 4.53 us -> none  [local(): labels = row_pixel[ordering].reshape(tile_count, per_peer)]
where the time goes in v3:
time: 158 us; the launch traced here: 157 us
  waiting for transfers between devices  55.9 us (35%)
  starting transfers between devices  48 us (30%)
  other arithmetic  33.2 us (21%)
  local copies, waits for them, and re-layouts  15.4 us (10%)
  matrix products  3.2 us (2%)
    ppermute x5, waiting for transfers between devices, tree_sum(): lax.ppermute(buf, axis, [(i, i ^ bit) for i in range(size)])  20.4 us
    ppermute x8, waiting for transfers between devices, from_behind(): return lax.ppermute(value, axis, pairs)  18.4 us
    all_to_all x1, waiting for transfers between devices, local(): lax.all_to_all(jnp.concatenate([outgoing, label_row], axis=1), ('face', '...  16.8 us
    all_to_all x1, starting transfers between devices, local(): lax.all_to_all(jnp.concatenate([outgoing, label_row], axis=1), ('face', '...  16.3 us
    ppermute x4, starting transfers between devices, tree_sum(): lax.ppermute(buf, axis, [(i, i ^ flip) for i in range(size)])  12.6 us
    ppermute x4, starting transfers between devices, tree_sum(): lax.ppermute(chunk_at(digit ^ flip), axis, pairs)  10.3 us
    ppermute x8, starting transfers between devices, from_behind(): return lax.ppermute(value, axis, pairs)  8.45 us
    scatter-add x1, other arithmetic, finish(): incoming = jnp.zeros((pixel_count + 1, channels), jnp.float32).at[send_pi...  6.52 us
  transfers between devices with their start and end apart: 22, of which 12 were waited for; matrix products, arithmetic and copies ran while one was open for 10% of the time, Pallas kernels for 0%

profile of v3, /device:TPU:1, one launch (start us, length us, event | category | flops | bytes accessed | tf_op | source)
XLA Modules:
  0.0 157.2 jit_solution(8431577268579927874)
XLA Ops:
  3.0 5.1 %sort.21 = (s32[1024]{0:T(1024)}, s32[1024]{0:T(1024)S(1)}, s32[1024]{0:T(1024)S(1)}) sort(s32[1024]{0:T(1024)} %param.19, s32[1024]{0:T(1024)S(1)} %iota.7, s32[1024]{0:T(1024)} %param.20), dimensions={0}, to_apply=%region_0.0 | sort | flops 10240 | bytes 24576 | tf_op jit(solution)/shard_map/sort | solution.py:198
  9.4 3.2 %gather_fusion = bf16[1024,128]{1,0:T(8,128)(2,1)S(1)} fusion(bf16[1024,128]{1,0:T(8,128)(2,1)S(1)} %bitcast.274, s32[1024]{0:T(1024)S(1)} %get-tuple-element.185), kind=kCustom, calls=%fused_computation | custom fusion | bytes 528384 | tf_op jit(solution)/shard_map/gather | solution.py:201
  12.6 0.9 pad_maximum_fusion
  13.5 16.3 %all-to-all-start = ((bf16[128,9,128]{2,1,0:T(8,128)(2,1)}), bf16[128,9,128]{2,1,0:T(8,128)(2,1)S(1)}, u32[]{:S(2)}, u32[]{:S(2)}) async-start(bf16[128,9,128]{2,1,0:T(8,128)(2,1)} %pad_maximum_fusion), calls=%async_computation | async-start | bytes 1048576 | tf_op jit(solution)/shard_map/all_to_all | solution.py:205
  30.0 16.8 %all-to-all-done = bf16[128,9,128]{2,1,0:T(8,128)(2,1)S(1)} async-done(((bf16[128,9,128]{2,1,0:T(8,128)(2,1)}), bf16[128,9,128]{2,1,0:T(8,128)(2,1)S(1)}, u32[]{:S(2)}, u32[]{:S(2)}) %all-to-all-start) | async-done | bytes 294944 | tf_op jit(solution)/shard_map/all_to_all | solution.py:205
  47.1 3.2 %scatter_custom_fusion = bf16[1024,128]{1,0:T(8,128)(2,1)S(1)} fusion(s32[1024]{0:T(1024)S(1)} %bitcast.289, bf16[128,9,128]{2,1,0:T(8,128)(2,1)S(1)} %all-to-all-done, bf16[]{:T(256)} %constant.58.clone.1), kind=kCustom, calls=%fused_computation.245 | custom fusion | bytes 524290 | tf_op jit(solution)/shard_map/scatter | solution.py:218
  50.4 1.9 %gather_fusion.1 = bf16[768,128]{1,0:T(8,128)(2,1)S(1)} fusion(bf16[1025,128]{1,0:T(8,128)(2,1)S(1)} %concatenate.47, s32[1024]{0:T(1024)S(1)} %pad_clamp_fusion.1), kind=kCustom, calls=%fused_computation.1 | custom fusion | bytes 396288 | tf_op jit(solution)/shard_map/gather | solution.py:232
  52.4 2.8 %collective-permute-start = (bf16[3,96,128]{2,1,0:T(8,128)(2,1)S(1)}, bf16[3,96,128]{2,1,0:T(8,128)(2,1)S(1)}, u32[]{:S(2)}, u32[]{:S(2)}) collective-permute-start(bf16[3,96,128]{2,1,0:T(8,128)(2,1)S(1)} %get-tuple-element.106), channel_id=1, source_target_pairs={{0,248},{8,0},{16,8},{24,16},{32,24},{40,32},{48,40},{56,48},{64,5... | collective-permute-start | bytes 221192 | tf_op jit(solution)/shard_map/ppermute | solution.py:15
  55.2 1.4 collective-permute-done
  56.6 5.1 %collective-permute-done.1 = bf16[3,96,128]{2,1,0:T(8,128)(2,1)S(1)} collective-permute-done((bf16[3,96,128]{2,1,0:T(8,128)(2,1)S(1)}, bf16[3,96,128]{2,1,0:T(8,128)(2,1)S(1)}, u32[]{:S(2)}, u32[]{:S(2)}) %collective-permute-start.1) | collective-permute-done | bytes 73760 | tf_op jit(solution)/shard_map/ppermute | solution.py:15
  61.8 3.3 %collective-permute-done.2 = bf16[3,96,128]{2,1,0:T(8,128)(2,1)S(1)} collective-permute-done((bf16[3,96,128]{2,1,0:T(8,128)(2,1)S(1)}, bf16[3,96,128]{2,1,0:T(8,128)(2,1)S(1)}, u32[]{:S(2)}, u32[]{:S(2)}) %collective-permute-start.2) | collective-permute-done | bytes 73760 | tf_op jit(solution)/shard_map/ppermute | solution.py:15
  65.7 4.1 %collective-permute-done.3 = bf16[3,96,128]{2,1,0:T(8,128)(2,1)S(1)} collective-permute-done((bf16[3,96,128]{2,1,0:T(8,128)(2,1)S(1)}, bf16[3,96,128]{2,1,0:T(8,128)(2,1)S(1)}, u32[]{:S(2)}, u32[]{:S(2)}) %collective-permute-start.3) | collective-permute-done | bytes 73760 | tf_op jit(solution)/shard_map/ppermute | solution.py:15
  70.0 1.5 gather_fusion.2
  72.1 3.8 %add_reduce_fusion = (f32[32,32]{1,0:T(8,128)S(1)}, f32[32,32,128]{2,1,0:T(8,128)S(1)}) fusion(f32[128]{0:T(128)S(1)} %copy-done.5, f32[128]{0:T(128)S(1)} %get-tuple-element.132, f32[38,38,128]{2,1,0:T(8,128)S(1)} %maximum_convert_fusion, f32[128]{0:T(128)S(1)} %get-tuple-element.133, f32[128]{0:T(128)S(1)} %get-tuple-element.134, ...), kind=kLoop, calls=%fused_computation.236 | loop fusion | flops 12975104 | bytes 26244096 | tf_op jit(solution)/shard_map/reduce_sum | solution.py:242
  80.6 0.9 multiply_reduce_fusion.1
  81.4 0.9 multiply_reduce_fusion.19
  82.6 1.0 fusion.107
  84.1 6.3 %collective-permute-start.4 = (f32[36352]{0:T(1024)S(1)}, f32[36352]{0:T(1024)S(1)}, u32[]{:S(2)}, u32[]{:S(2)}) collective-permute-start(f32[36352]{0:T(1024)S(1)} %slice_select_fusion), channel_id=1, source_target_pairs={{0,1},{1,0},{2,3},{3,2},{4,5},{5,4},{6,7},{7,6},{8,9},{9,8},{10,11... | collective-permute-start | bytes 436232 | tf_op jit(solution)/shard_map/ppermute | solution.py:60
  90.4 6.1 %fusion.137 = (bf16[38,38,128]{2,1,0:T(8,128)(2,1)S(1)}, f32[38,38,128]{2,1,0:T(8,128)S(1)}) fusion(f32[128]{0:T(128)S(1)} %get-tuple-element.131, f32[128]{0:T(128)S(1)} %get-tuple-element.150, f32[128]{0:T(128)S(1)} %get-tuple-element.169, f32[128]{0:T(128)S(1)} %get-tuple-element.179, f32[128]{0:T(128)S(1)} %get-tuple-element.178, ...), kind=kLoop, calls=%fused_computation.401 | loop fusion | flops 18113536 | bytes 1658368 | tf_op jit(solution)/shard_map/convert.15
  96.7 1.6 %scatter_custom_fusion.1 = bf16[769,128]{1,0:T(8,128)(2,1)S(1)} fusion(s32[420]{0:T(512)S(1)} %bitcast.286, bf16[114,128]{1,0:T(8,128)(2,1)S(1)} %reshape.362, bf16[]{:T(256)} %constant.170, bf16[192,128]{1,0:T(8,128)(2,1)S(1)} %reshape.361, bf16[114,128]{1,0:T(8,128)(2,1)S(1)} %reshape.360, bf16[]{:T(256)} %constant.58.clone.1), kind=kCustom, calls=%fused_computation.255 | custom fusion | flops 322560 | bytes 307460 | tf_op jit(solution)/shard_map/scatter | solution.py:283
  98.9 3.6 %collective-permute-start.6 = (f32[9088]{0:T(1024)S(1)}, f32[9088]{0:T(1024)S(1)}, u32[]{:S(2)}, u32[]{:S(2)}) collective-permute-start(f32[9088]{0:T(1024)S(1)} %get-tuple-element.118), channel_id=1, source_target_pairs={{0,4},{2,6},{4,0},{6,2},{1,5},{3,7},{5,1},{7,3},{8,12},{10,14},{12... | collective-permute-start | bytes 109064 | tf_op jit(solution)/shard_map/ppermute | solution.py:60
  102.6 4.8 %collective-permute-start.10 = (bf16[3,96,128]{2,1,0:T(8,128)(2,1)S(1)}, bf16[3,96,128]{2,1,0:T(8,128)(2,1)S(1)}, u32[]{:S(2)}, u32[]{:S(2)}) collective-permute-start(bf16[3,96,128]{2,1,0:T(8,128)(2,1)S(1)} %get-tuple-element.103), channel_id=1, source_target_pairs={{0,248},{8,0},{16,8},{24,16},{32,24},{40,32},{48,40},{56,48},{64,5... | collective-permute-start | bytes 221192 | tf_op jit(solution)/shard_map/ppermute | solution.py:15
  107.6 3.1 %collective-permute-done.8 = f32[9088]{0:T(1024)S(1)} collective-permute-done((f32[9088]{0:T(1024)S(1)}, f32[9088]{0:T(1024)S(1)}, u32[]{:S(2)}, u32[]{:S(2)}) %collective-permute-start.8) | collective-permute-done | bytes 36384 | tf_op jit(solution)/shard_map/ppermute | solution.py:63
  110.8 4.4 %collective-permute-done.13 = bf16[3,96,128]{2,1,0:T(8,128)(2,1)S(1)} collective-permute-done((bf16[3,96,128]{2,1,0:T(8,128)(2,1)S(1)}, bf16[3,96,128]{2,1,0:T(8,128)(2,1)S(1)}, u32[]{:S(2)}, u32[]{:S(2)}) %collective-permute-start.13) | collective-permute-done | bytes 73760 | tf_op jit(solution)/shard_map/ppermute | solution.py:15
  115.4 3.7 %collective-permute-done.11 = f32[9088]{0:T(1024)S(1)} collective-permute-done((f32[9088]{0:T(1024)S(1)}, f32[9088]{0:T(1024)S(1)}, u32[]{:S(2)}, u32[]{:S(2)}) %collective-permute-start.11) | collective-permute-done | bytes 36384 | tf_op jit(solution)/shard_map/ppermute | solution.py:63
  119.2 6.7 %collective-permute-done.12 = f32[9088]{0:T(1024)S(1)} collective-permute-done((f32[9088]{0:T(1024)S(1)}, f32[9088]{0:T(1024)S(1)}, u32[]{:S(2)}, u32[]{:S(2)}) %collective-permute-start.12) | collective-permute-done | bytes 36384 | tf_op jit(solution)/shard_map/ppermute | solution.py:63
  126.1 2.7 %collective-permute-done.15 = f32[9088]{0:T(1024)S(1)} collective-permute-done((f32[9088]{0:T(1024)S(1)}, f32[9088]{0:T(1024)S(1)}, u32[]{:S(2)}, u32[]{:S(2)}) %collective-permute-start.15) | collective-permute-done | bytes 36384 | tf_op jit(solution)/shard_map/ppermute | solution.py:63
  129.0 4.2 %collective-permute-done.16 = f32[9088]{0:T(1024)S(1)} collective-permute-done((f32[9088]{0:T(1024)S(1)}, f32[9088]{0:T(1024)S(1)}, u32[]{:S(2)}, u32[]{:S(2)}) %collective-permute-start.16) | collective-permute-done | bytes 36384 | tf_op jit(solution)/shard_map/ppermute | solution.py:63
  133.2 3.4 %collective-permute-start.18 = (f32[9088]{0:T(1024)S(1)}, f32[9088]{0:T(1024)S(1)}, u32[]{:S(2)}, u32[]{:S(2)}) collective-permute-start(f32[9088]{0:T(1024)S(1)} %add.630), channel_id=1, source_target_pairs={{0,4},{2,6},{4,0},{6,2},{1,5},{3,7},{5,1},{7,3},{8,12},{10,14},{12... | collective-permute-start | bytes 109064 | tf_op jit(solution)/shard_map/ppermute | solution.py:68
  136.7 6.5 %scatter_custom_fusion.2 = f32[1025,128]{1,0:T(8,128)S(1)} fusion(s32[768]{0:T(1024)S(1)} %fusion.131, bf16[768,128]{1,0:T(8,128)(2,1)S(1)} %bitcast.281, f32[]{:T(128)} %constant.131.clone.1), kind=kCustom, calls=%fused_computation.238 | custom fusion | flops 196608 | bytes 721412 | tf_op jit(solution)/shard_map/scatter-add | solution.py:292
  143.3 9.2 %collective-permute-start.20 = (f32[36352]{0:T(1024)S(1)}, f32[36352]{0:T(1024)S(1)}, u32[]{:S(2)}, u32[]{:S(2)}) collective-permute-start(f32[36352]{0:T(1024)S(1)} %pad_maximum_fusion.2), channel_id=1, source_target_pairs={{0,1},{1,0},{2,3},{3,2},{4,5},{5,4},{6,7},{7,6},{8,9},{9,8},{10,11... | collective-permute-start | bytes 436232 | tf_op jit(solution)/shard_map/ppermute | solution.py:68
  152.5 0.8 fusion.106
  (182 shorter events, 16.2 us)
Async XLA Ops:
  0.6 8.7 %copy-start = (bf16[1,1024,128]{2,1,0:T(8,128)(2,1)S(1)}, bf16[1,1024,128]{2,1,0:T(8,128)(2,1)}, u32[]{:S(2)}) copy-start(bf16[1,1024,128]{2,1,0:T(8,128)(2,1)} %param.18) | copy-start | bytes 786436
  12.6 17.3 %copy-start.3 = (s32[1,8,96]{2,1,0:T(8,128)S(1)}, s32[1,8,96]{2,1,0:T(8,128)}, u32[]{:S(2)}) copy-start(s32[1,8,96]{2,1,0:T(8,128)} %param.22) | copy-start | bytes 9220
  12.6 17.4 %copy-start.4 = (bf16[49,128]{1,0:T(8,128)(2,1)S(1)}, bf16[49,128]{1,0:T(8,128)(2,1)}, u32[]{:S(2)}) copy-start(bf16[49,128]{1,0:T(8,128)(2,1)} %param.25) | copy-start | bytes 37636
  12.6 17.4 %copy-start.11 = (s32[1,8]{1,0:T(1,128)S(1)}, s32[1,8]{1,0:T(1,128)}, u32[]{:S(2)}) copy-start(s32[1,8]{1,0:T(1,128)} %param.21) | copy-start | bytes 100
  13.5 33.4 %all-to-all-start = ((bf16[128,9,128]{2,1,0:T(8,128)(2,1)}), bf16[128,9,128]{2,1,0:T(8,128)(2,1)S(1)}, u32[]{:S(2)}, u32[]{:S(2)}) async-start(bf16[128,9,128]{2,1,0:T(8,128)(2,1)} %pad_maximum_fusion), calls=%async_computation | async-start | bytes 1048576 | tf_op jit(solution)/shard_map/all_to_all | solution.py:205
  52.4 4.2 %collective-permute-start = (bf16[3,96,128]{2,1,0:T(8,128)(2,1)S(1)}, bf16[3,96,128]{2,1,0:T(8,128)(2,1)S(1)}, u32[]{:S(2)}, u32[]{:S(2)}) collective-permute-start(bf16[3,96,128]{2,1,0:T(8,128)(2,1)S(1)} %get-tuple-element.106), channel_id=1, source_target_pairs={{0,248},{8,0},{16,8},{24,16},{32,24},{40,32},{48,40},{56,48},{64,5... | collective-permute-start | bytes 221192 | tf_op jit(solution)/shard_map/ppermute | solution.py:15
  55.2 6.5 %collective-permute-start.1 = (bf16[3,96,128]{2,1,0:T(8,128)(2,1)S(1)}, bf16[3,96,128]{2,1,0:T(8,128)(2,1)S(1)}, u32[]{:S(2)}, u32[]{:S(2)}) collective-permute-start(bf16[3,96,128]{2,1,0:T(8,128)(2,1)S(1)} %get-tuple-element.107), channel_id=1, source_target_pairs={{0,8},{8,16},{16,24},{24,32},{32,40},{40,48},{48,56},{56,64},{64,7... | collective-permute-start | bytes 221192 | tf_op jit(solution)/shard_map/ppermute | solution.py:15
  61.7 3.4 %collective-permute-start.2 = (bf16[3,96,128]{2,1,0:T(8,128)(2,1)S(1)}, bf16[3,96,128]{2,1,0:T(8,128)(2,1)S(1)}, u32[]{:S(2)}, u32[]{:S(2)}) collective-permute-start(bf16[3,96,128]{2,1,0:T(8,128)(2,1)S(1)} %pad_maximum_fusion.4), channel_id=1, source_target_pairs={{0,6},{2,0},{4,2},{6,4},{1,7},{3,1},{5,3},{7,5},{8,14},{10,8},{12,... | collective-permute-start | bytes 221192 | tf_op jit(solution)/shard_map/ppermute | solution.py:15
  65.2 4.7 %collective-permute-start.3 = (bf16[3,96,128]{2,1,0:T(8,128)(2,1)S(1)}, bf16[3,96,128]{2,1,0:T(8,128)(2,1)S(1)}, u32[]{:S(2)}, u32[]{:S(2)}) collective-permute-start(bf16[3,96,128]{2,1,0:T(8,128)(2,1)S(1)} %pad_maximum_fusion.5), channel_id=1, source_target_pairs={{0,2},{2,4},{4,6},{6,0},{1,3},{3,5},{5,7},{7,1},{8,10},{10,12},{12... | collective-permute-start | bytes 221192 | tf_op jit(solution)/shard_map/ppermute | solution.py:15
  75.9 0.9 copy-start.7
  75.9 0.9 copy-start.8
  76.8 1.0 copy-start.1
  76.8 0.9 copy-start.9
  76.9 0.9 copy-start.10
  81.4 1.2 copy-start.12
  84.1 14.3 %collective-permute-start.4 = (f32[36352]{0:T(1024)S(1)}, f32[36352]{0:T(1024)S(1)}, u32[]{:S(2)}, u32[]{:S(2)}) collective-permute-start(f32[36352]{0:T(1024)S(1)} %slice_select_fusion), channel_id=1, source_target_pairs={{0,1},{1,0},{2,3},{3,2},{4,5},{5,4},{6,7},{7,6},{8,9},{9,8},{10,11... | collective-permute-start | bytes 436232 | tf_op jit(solution)/shard_map/ppermute | solution.py:60
  98.5 8.9 %collective-permute-start.7 = (f32[9088]{0:T(1024)S(1)}, f32[9088]{0:T(1024)S(1)}, u32[]{:S(2)}, u32[]{:S(2)}) collective-permute-start(f32[9088]{0:T(1024)S(1)} %select_select_fusion.4), channel_id=1, source_target_pairs={{0,6},{2,4},{4,2},{6,0},{1,7},{3,5},{5,3},{7,1},{8,14},{10,12},{12... | collective-permute-start | bytes 109064 | tf_op jit(solution)/shard_map/ppermute | solution.py:60
  98.8 8.6 %collective-permute-start.5 = (f32[9088]{0:T(1024)S(1)}, f32[9088]{0:T(1024)S(1)}, u32[]{:S(2)}, u32[]{:S(2)}) collective-permute-start(f32[9088]{0:T(1024)S(1)} %get-tuple-element.117), channel_id=1, source_target_pairs={{0,2},{2,0},{4,6},{6,4},{1,3},{3,1},{5,7},{7,5},{8,10},{10,8},{12,... | collective-permute-start | bytes 109064 | tf_op jit(solution)/shard_map/ppermute | solution.py:60
  98.9 8.5 %collective-permute-start.6 = (f32[9088]{0:T(1024)S(1)}, f32[9088]{0:T(1024)S(1)}, u32[]{:S(2)}, u32[]{:S(2)}) collective-permute-start(f32[9088]{0:T(1024)S(1)} %get-tuple-element.118), channel_id=1, source_target_pairs={{0,4},{2,6},{4,0},{6,2},{1,5},{3,7},{5,1},{7,3},{8,12},{10,14},{12... | collective-permute-start | bytes 109064 | tf_op jit(solution)/shard_map/ppermute | solution.py:60
  102.5 8.1 %collective-permute-start.9 = (bf16[3,96,128]{2,1,0:T(8,128)(2,1)S(1)}, bf16[3,96,128]{2,1,0:T(8,128)(2,1)S(1)}, u32[]{:S(2)}, u32[]{:S(2)}) collective-permute-start(bf16[3,96,128]{2,1,0:T(8,128)(2,1)S(1)} %get-tuple-element.102), channel_id=1, source_target_pairs={{0,8},{8,16},{16,24},{24,32},{32,40},{40,48},{48,56},{56,64},{64,7... | collective-permute-start | bytes 221192 | tf_op jit(solution)/shard_map/ppermute | solution.py:15
  102.6 8.0 %collective-permute-start.10 = (bf16[3,96,128]{2,1,0:T(8,128)(2,1)S(1)}, bf16[3,96,128]{2,1,0:T(8,128)(2,1)S(1)}, u32[]{:S(2)}, u32[]{:S(2)}) collective-permute-start(bf16[3,96,128]{2,1,0:T(8,128)(2,1)S(1)} %get-tuple-element.103), channel_id=1, source_target_pairs={{0,248},{8,0},{16,8},{24,16},{32,24},{40,32},{48,40},{56,48},{64,5... | collective-permute-start | bytes 221192 | tf_op jit(solution)/shard_map/ppermute | solution.py:15
  107.4 3.2 %collective-permute-start.8 = (f32[9088]{0:T(1024)S(1)}, f32[9088]{0:T(1024)S(1)}, u32[]{:S(2)}, u32[]{:S(2)}) collective-permute-start(f32[9088]{0:T(1024)S(1)} %add_add_fusion), channel_id=1, source_target_pairs={{0,8},{8,0},{16,24},{24,16},{32,40},{40,32},{48,56},{56,48},{64,72... | collective-permute-start | bytes 109064 | tf_op jit(solution)/shard_map/ppermute | solution.py:63
  110.7 4.5 %collective-permute-start.13 = (bf16[3,96,128]{2,1,0:T(8,128)(2,1)S(1)}, bf16[3,96,128]{2,1,0:T(8,128)(2,1)S(1)}, u32[]{:S(2)}, u32[]{:S(2)}) collective-permute-start(bf16[3,96,128]{2,1,0:T(8,128)(2,1)S(1)} %pad_maximum_fusion.6), channel_id=1, source_target_pairs={{0,2},{2,4},{4,6},{6,0},{1,3},{3,5},{5,7},{7,1},{8,10},{10,12},{12... | collective-permute-start | bytes 221192 | tf_op jit(solution)/shard_map/ppermute | solution.py:15
  115.3 10.6 %collective-permute-start.14 = (bf16[3,96,128]{2,1,0:T(8,128)(2,1)S(1)}, bf16[3,96,128]{2,1,0:T(8,128)(2,1)S(1)}, u32[]{:S(2)}, u32[]{:S(2)}) collective-permute-start(bf16[3,96,128]{2,1,0:T(8,128)(2,1)S(1)} %pad_maximum_fusion.7), channel_id=1, source_target_pairs={{0,6},{2,0},{4,2},{6,4},{1,7},{3,1},{5,3},{7,5},{8,14},{10,8},{12,... | collective-permute-start | bytes 221192 | tf_op jit(solution)/shard_map/ppermute | solution.py:15
  115.3 3.8 %collective-permute-start.11 = (f32[9088]{0:T(1024)S(1)}, f32[9088]{0:T(1024)S(1)}, u32[]{:S(2)}, u32[]{:S(2)}) collective-permute-start(f32[9088]{0:T(1024)S(1)} %add.625), channel_id=1, source_target_pairs={{0,16},{8,24},{16,0},{24,8},{32,48},{40,56},{48,32},{56,40},{64,80... | collective-permute-start | bytes 109064 | tf_op jit(solution)/shard_map/ppermute | solution.py:63
  119.2 6.7 %collective-permute-start.12 = (f32[9088]{0:T(1024)S(1)}, f32[9088]{0:T(1024)S(1)}, u32[]{:S(2)}, u32[]{:S(2)}) collective-permute-start(f32[9088]{0:T(1024)S(1)} %add.626), channel_id=1, source_target_pairs={{0,32},{8,40},{16,48},{24,56},{32,0},{40,8},{48,16},{56,24},{64,96... | collective-permute-start | bytes 109064 | tf_op jit(solution)/shard_map/ppermute | solution.py:63
  126.0 2.9 %collective-permute-start.15 = (f32[9088]{0:T(1024)S(1)}, f32[9088]{0:T(1024)S(1)}, u32[]{:S(2)}, u32[]{:S(2)}) collective-permute-start(f32[9088]{0:T(1024)S(1)} %add.627), channel_id=1, source_target_pairs={{0,64},{8,72},{16,80},{24,88},{32,96},{40,104},{48,112},{56,120},{... | collective-permute-start | bytes 109064 | tf_op jit(solution)/shard_map/ppermute | solution.py:63
  128.9 4.3 %collective-permute-start.16 = (f32[9088]{0:T(1024)S(1)}, f32[9088]{0:T(1024)S(1)}, u32[]{:S(2)}, u32[]{:S(2)}) collective-permute-start(f32[9088]{0:T(1024)S(1)} %add.629), channel_id=1, source_target_pairs={{0,128},{8,136},{16,144},{24,152},{32,160},{40,168},{48,176},{56,1... | collective-permute-start | bytes 109064 | tf_op jit(solution)/shard_map/ppermute | solution.py:63
  133.2 10.0 %collective-permute-start.19 = (f32[9088]{0:T(1024)S(1)}, f32[9088]{0:T(1024)S(1)}, u32[]{:S(2)}, u32[]{:S(2)}) collective-permute-start(f32[9088]{0:T(1024)S(1)} %add.630), channel_id=1, source_target_pairs={{0,6},{2,4},{4,2},{6,0},{1,7},{3,5},{5,3},{7,1},{8,14},{10,12},{12... | collective-permute-start | bytes 109064 | tf_op jit(solution)/shard_map/ppermute | solution.py:68
  133.2 10.0 %collective-permute-start.18 = (f32[9088]{0:T(1024)S(1)}, f32[9088]{0:T(1024)S(1)}, u32[]{:S(2)}, u32[]{:S(2)}) collective-permute-start(f32[9088]{0:T(1024)S(1)} %add.630), channel_id=1, source_target_pairs={{0,4},{2,6},{4,0},{6,2},{1,5},{3,7},{5,1},{7,3},{8,12},{10,14},{12... | collective-permute-start | bytes 109064 | tf_op jit(solution)/shard_map/ppermute | solution.py:68
  136.6 6.6 %collective-permute-start.17 = (f32[9088]{0:T(1024)S(1)}, f32[9088]{0:T(1024)S(1)}, u32[]{:S(2)}, u32[]{:S(2)}) collective-permute-start(f32[9088]{0:T(1024)S(1)} %add.630), channel_id=1, source_target_pairs={{0,2},{2,0},{4,6},{6,4},{1,3},{3,1},{5,7},{7,5},{8,10},{10,8},{12,... | collective-permute-start | bytes 109064 | tf_op jit(solution)/shard_map/ppermute | solution.py:68
  143.3 10.2 %collective-permute-start.20 = (f32[36352]{0:T(1024)S(1)}, f32[36352]{0:T(1024)S(1)}, u32[]{:S(2)}, u32[]{:S(2)}) collective-permute-start(f32[36352]{0:T(1024)S(1)} %pad_maximum_fusion.2), channel_id=1, source_target_pairs={{0,1},{1,0},{2,3},{3,2},{4,5},{5,4},{6,7},{7,6},{8,9},{9,8},{10,11... | collective-permute-start | bytes 436232 | tf_op jit(solution)/shard_map/ppermute | solution.py:68
  (3 other events, 2.5 us)

commit v4 on v3

--- a/solution.py
+++ b/solution.py
@@ -286,10 +286,11 @@
 
     def finish(moved):
         returned = jnp.where(live, moved, jnp.zeros((), moved.dtype))
-        incoming = (
-            jnp.zeros((pixel_count + 1, channels), jnp.float32)
-            .at[send_pixels[0].reshape(-1)]
-            .add(returned.reshape(-1, channels).astype(jnp.float32))
+        spread = (
+            jnp.arange(pixel_count + 1, dtype=jnp.int32)[:, None] == send_pixels[0].reshape(1, -1)
+        ).astype(returned.dtype)
+        incoming = jnp.dot(
+            spread, returned.reshape(-1, channels), preferred_element_type=jnp.float32
         )
         return (grad_f + inner_grad + incoming[:pixel_count]).astype(jnp.bfloat16)
 

time: 158 us -> 155 us (0.981)
  other arithmetic: 33.2 us -> 25.9 us
  waiting for transfers between devices: 55.9 us -> 58.4 us
    scatter-add x1 -> x0, other arithmetic: 6.52 us -> none  [finish(): incoming = jnp.zeros((pixel_count + 1, channels), jnp.float32).at[send_pi...]
    ppermute x4, waiting for transfers between devices: 0.23 us -> 2.72 us  [tree_sum(): lax.ppermute(buf, axis, [(i, i ^ flip) for i in range(size)])]
  transfers between devices with their start and end apart: 22 -> 22, of which waited for: 12 -> 14; matrix products, arithmetic and copies ran while one was open for 10% -> 6% of each run, Pallas kernels for 0% -> 0%
where the time goes in v4:
time: 155 us
  waiting for transfers between devices  58.4 us (38%)
  starting transfers between devices  49 us (32%)
  other arithmetic  25.9 us (17%)
  local copies, waits for them, and re-layouts  15.4 us (10%)
  matrix products  4.63 us (3%)
    ppermute x5, waiting for transfers between devices, tree_sum(): lax.ppermute(buf, axis, [(i, i ^ bit) for i in range(size)])  20.4 us
    ppermute x8, waiting for transfers between devices, from_behind(): return lax.ppermute(value, axis, pairs)  18.4 us
    all_to_all x1, waiting for transfers between devices, local(): lax.all_to_all(jnp.concatenate([outgoing, label_row], axis=1), ('face', '...  16.8 us
    all_to_all x1, starting transfers between devices, local(): lax.all_to_all(jnp.concatenate([outgoing, label_row], axis=1), ('face', '...  16.3 us
    ppermute x4, starting transfers between devices, tree_sum(): lax.ppermute(buf, axis, [(i, i ^ flip) for i in range(size)])  13.6 us
    ppermute x4, starting transfers between devices, tree_sum(): lax.ppermute(chunk_at(digit ^ flip), axis, pairs)  10.3 us
    ppermute x8, starting transfers between devices, from_behind(): return lax.ppermute(value, axis, pairs)  8.45 us
    another operation x3, other arithmetic  6.16 us
  transfers between devices with their start and end apart: 22, of which 14 were waited for; matrix products, arithmetic and copies ran while one was open for 6% of the time, Pallas kernels for 0%

profile of v4, /device:TPU:1, one launch (start us, length us, event | category | flops | bytes accessed | tf_op | source)
XLA Modules:
  0.0 154.7 jit_solution(18104589696996939340)
XLA Ops:
  3.0 5.1 %sort.21 = (s32[1024]{0:T(1024)}, s32[1024]{0:T(1024)S(1)}, s32[1024]{0:T(1024)S(1)}) sort(s32[1024]{0:T(1024)} %param.19, s32[1024]{0:T(1024)S(1)} %iota.11, s32[1024]{0:T(1024)} %param.20), dimensions={0}, to_apply=%region_0.0 | sort | flops 10240 | bytes 24576 | tf_op jit(solution)/shard_map/sort | solution.py:198
  9.4 3.2 %gather_fusion = bf16[1024,128]{1,0:T(8,128)(2,1)S(1)} fusion(bf16[1024,128]{1,0:T(8,128)(2,1)S(1)} %bitcast.274, s32[1024]{0:T(1024)S(1)} %get-tuple-element.185), kind=kCustom, calls=%fused_computation | custom fusion | bytes 528384 | tf_op jit(solution)/shard_map/gather | solution.py:201
  12.6 0.9 pad_maximum_fusion
  13.5 16.3 %all-to-all-start = ((bf16[128,9,128]{2,1,0:T(8,128)(2,1)}), bf16[128,9,128]{2,1,0:T(8,128)(2,1)S(1)}, u32[]{:S(2)}, u32[]{:S(2)}) async-start(bf16[128,9,128]{2,1,0:T(8,128)(2,1)} %pad_maximum_fusion), calls=%async_computation | async-start | bytes 1048576 | tf_op jit(solution)/shard_map/all_to_all | solution.py:205
  30.0 16.8 %all-to-all-done = bf16[128,9,128]{2,1,0:T(8,128)(2,1)S(1)} async-done(((bf16[128,9,128]{2,1,0:T(8,128)(2,1)}), bf16[128,9,128]{2,1,0:T(8,128)(2,1)S(1)}, u32[]{:S(2)}, u32[]{:S(2)}) %all-to-all-start) | async-done | bytes 294944 | tf_op jit(solution)/shard_map/all_to_all | solution.py:205
  47.1 3.2 %scatter_custom_fusion = bf16[1024,128]{1,0:T(8,128)(2,1)S(1)} fusion(s32[1024]{0:T(1024)S(1)} %bitcast.289, bf16[128,9,128]{2,1,0:T(8,128)(2,1)S(1)} %all-to-all-done, bf16[]{:T(256)} %constant.63.clone.1), kind=kCustom, calls=%fused_computation.246 | custom fusion | bytes 524290 | tf_op jit(solution)/shard_map/scatter | solution.py:218
  50.4 1.9 %gather_fusion.1 = bf16[768,128]{1,0:T(8,128)(2,1)S(1)} fusion(bf16[1025,128]{1,0:T(8,128)(2,1)S(1)} %concatenate.47, s32[1024]{0:T(1024)S(1)} %pad_clamp_fusion.1), kind=kCustom, calls=%fused_computation.1 | custom fusion | bytes 396288 | tf_op jit(solution)/shard_map/gather | solution.py:232
  52.4 2.8 %collective-permute-start = (bf16[3,96,128]{2,1,0:T(8,128)(2,1)S(1)}, bf16[3,96,128]{2,1,0:T(8,128)(2,1)S(1)}, u32[]{:S(2)}, u32[]{:S(2)}) collective-permute-start(bf16[3,96,128]{2,1,0:T(8,128)(2,1)S(1)} %get-tuple-element.106), channel_id=1, source_target_pairs={{0,248},{8,0},{16,8},{24,16},{32,24},{40,32},{48,40},{56,48},{64,5... | collective-permute-start | bytes 221192 | tf_op jit(solution)/shard_map/ppermute | solution.py:15
  55.2 1.4 collective-permute-done
  56.6 5.1 %collective-permute-done.1 = bf16[3,96,128]{2,1,0:T(8,128)(2,1)S(1)} collective-permute-done((bf16[3,96,128]{2,1,0:T(8,128)(2,1)S(1)}, bf16[3,96,128]{2,1,0:T(8,128)(2,1)S(1)}, u32[]{:S(2)}, u32[]{:S(2)}) %collective-permute-start.1) | collective-permute-done | bytes 73760 | tf_op jit(solution)/shard_map/ppermute | solution.py:15
  61.8 3.3 %collective-permute-done.2 = bf16[3,96,128]{2,1,0:T(8,128)(2,1)S(1)} collective-permute-done((bf16[3,96,128]{2,1,0:T(8,128)(2,1)S(1)}, bf16[3,96,128]{2,1,0:T(8,128)(2,1)S(1)}, u32[]{:S(2)}, u32[]{:S(2)}) %collective-permute-start.2) | collective-permute-done | bytes 73760 | tf_op jit(solution)/shard_map/ppermute | solution.py:15
  65.8 4.1 %collective-permute-done.3 = bf16[3,96,128]{2,1,0:T(8,128)(2,1)S(1)} collective-permute-done((bf16[3,96,128]{2,1,0:T(8,128)(2,1)S(1)}, bf16[3,96,128]{2,1,0:T(8,128)(2,1)S(1)}, u32[]{:S(2)}, u32[]{:S(2)}) %collective-permute-start.3) | collective-permute-done | bytes 73760 | tf_op jit(solution)/shard_map/ppermute | solution.py:15
  70.0 1.5 gather_fusion.2
  72.1 3.8 %add_reduce_fusion = (f32[32,32]{1,0:T(8,128)S(1)}, f32[32,32,128]{2,1,0:T(8,128)S(1)}) fusion(f32[128]{0:T(128)S(1)} %copy-done.5, f32[128]{0:T(128)S(1)} %get-tuple-element.132, f32[38,38,128]{2,1,0:T(8,128)S(1)} %maximum_convert_fusion, f32[128]{0:T(128)S(1)} %get-tuple-element.133, f32[128]{0:T(128)S(1)} %get-tuple-element.134, ...), kind=kLoop, calls=%fused_computation.240 | loop fusion | flops 12975104 | bytes 26244096 | tf_op jit(solution)/shard_map/reduce_sum | solution.py:242
  80.6 0.9 multiply_reduce_fusion.1
  81.4 0.9 multiply_reduce_fusion.19
  82.7 1.0 fusion.111
  84.1 6.3 %collective-permute-start.4 = (f32[36352]{0:T(1024)S(1)}, f32[36352]{0:T(1024)S(1)}, u32[]{:S(2)}, u32[]{:S(2)}) collective-permute-start(f32[36352]{0:T(1024)S(1)} %slice_select_fusion), channel_id=1, source_target_pairs={{0,1},{1,0},{2,3},{3,2},{4,5},{5,4},{6,7},{7,6},{8,9},{9,8},{10,11... | collective-permute-start | bytes 436232 | tf_op jit(solution)/shard_map/ppermute | solution.py:60
  90.4 6.1 %fusion.138 = (bf16[38,38,128]{2,1,0:T(8,128)(2,1)S(1)}, f32[38,38,128]{2,1,0:T(8,128)S(1)}) fusion(f32[128]{0:T(128)S(1)} %get-tuple-element.131, f32[128]{0:T(128)S(1)} %get-tuple-element.150, f32[128]{0:T(128)S(1)} %get-tuple-element.169, f32[128]{0:T(128)S(1)} %get-tuple-element.179, f32[128]{0:T(128)S(1)} %get-tuple-element.178, ...), kind=kLoop, calls=%fused_computation.401 | loop fusion | flops 18113536 | bytes 1658368 | tf_op jit(solution)/shard_map/convert.14
  96.8 1.6 %scatter_custom_fusion.1 = bf16[769,128]{1,0:T(8,128)(2,1)S(1)} fusion(s32[420]{0:T(512)S(1)} %bitcast.286, bf16[114,128]{1,0:T(8,128)(2,1)S(1)} %reshape.335, bf16[]{:T(256)} %constant.166, bf16[192,128]{1,0:T(8,128)(2,1)S(1)} %reshape.334, bf16[114,128]{1,0:T(8,128)(2,1)S(1)} %reshape.333, bf16[]{:T(256)} %constant.63.clone.1), kind=kCustom, calls=%fused_computation.256 | custom fusion | flops 322560 | bytes 307460 | tf_op jit(solution)/shard_map/scatter | solution.py:283
  98.9 3.6 %collective-permute-start.6 = (f32[9088]{0:T(1024)S(1)}, f32[9088]{0:T(1024)S(1)}, u32[]{:S(2)}, u32[]{:S(2)}) collective-permute-start(f32[9088]{0:T(1024)S(1)} %get-tuple-element.118), channel_id=1, source_target_pairs={{0,4},{2,6},{4,0},{6,2},{1,5},{3,7},{5,1},{7,3},{8,12},{10,14},{12... | collective-permute-start | bytes 109064 | tf_op jit(solution)/shard_map/ppermute | solution.py:60
  102.6 4.8 %collective-permute-start.10 = (bf16[3,96,128]{2,1,0:T(8,128)(2,1)S(1)}, bf16[3,96,128]{2,1,0:T(8,128)(2,1)S(1)}, u32[]{:S(2)}, u32[]{:S(2)}) collective-permute-start(bf16[3,96,128]{2,1,0:T(8,128)(2,1)S(1)} %get-tuple-element.103), channel_id=1, source_target_pairs={{0,248},{8,0},{16,8},{24,16},{32,24},{40,32},{48,40},{56,48},{64,5... | collective-permute-start | bytes 221192 | tf_op jit(solution)/shard_map/ppermute | solution.py:15
  107.6 3.1 %collective-permute-done.8 = f32[9088]{0:T(1024)S(1)} collective-permute-done((f32[9088]{0:T(1024)S(1)}, f32[9088]{0:T(1024)S(1)}, u32[]{:S(2)}, u32[]{:S(2)}) %collective-permute-start.8) | collective-permute-done | bytes 36384 | tf_op jit(solution)/shard_map/ppermute | solution.py:63
  110.8 4.4 %collective-permute-done.13 = bf16[3,96,128]{2,1,0:T(8,128)(2,1)S(1)} collective-permute-done((bf16[3,96,128]{2,1,0:T(8,128)(2,1)S(1)}, bf16[3,96,128]{2,1,0:T(8,128)(2,1)S(1)}, u32[]{:S(2)}, u32[]{:S(2)}) %collective-permute-start.13) | collective-permute-done | bytes 73760 | tf_op jit(solution)/shard_map/ppermute | solution.py:15
  115.5 3.7 %collective-permute-done.11 = f32[9088]{0:T(1024)S(1)} collective-permute-done((f32[9088]{0:T(1024)S(1)}, f32[9088]{0:T(1024)S(1)}, u32[]{:S(2)}, u32[]{:S(2)}) %collective-permute-start.11) | collective-permute-done | bytes 36384 | tf_op jit(solution)/shard_map/ppermute | solution.py:63
  119.2 6.7 %collective-permute-done.12 = f32[9088]{0:T(1024)S(1)} collective-permute-done((f32[9088]{0:T(1024)S(1)}, f32[9088]{0:T(1024)S(1)}, u32[]{:S(2)}, u32[]{:S(2)}) %collective-permute-start.12) | collective-permute-done | bytes 36384 | tf_op jit(solution)/shard_map/ppermute | solution.py:63
  126.1 2.8 %collective-permute-done.15 = f32[9088]{0:T(1024)S(1)} collective-permute-done((f32[9088]{0:T(1024)S(1)}, f32[9088]{0:T(1024)S(1)}, u32[]{:S(2)}, u32[]{:S(2)}) %collective-permute-start.15) | collective-permute-done | bytes 36384 | tf_op jit(solution)/shard_map/ppermute | solution.py:63
  129.0 4.2 %collective-permute-done.16 = f32[9088]{0:T(1024)S(1)} collective-permute-done((f32[9088]{0:T(1024)S(1)}, f32[9088]{0:T(1024)S(1)}, u32[]{:S(2)}, u32[]{:S(2)}) %collective-permute-start.16) | collective-permute-done | bytes 36384 | tf_op jit(solution)/shard_map/ppermute | solution.py:63
  133.2 3.4 %collective-permute-start.18 = (f32[9088]{0:T(1024)S(1)}, f32[9088]{0:T(1024)S(1)}, u32[]{:S(2)}, u32[]{:S(2)}) collective-permute-start(f32[9088]{0:T(1024)S(1)} %add.613), channel_id=1, source_target_pairs={{0,4},{2,6},{4,0},{6,2},{1,5},{3,7},{5,1},{7,3},{8,12},{10,14},{12... | collective-permute-start | bytes 109064 | tf_op jit(solution)/shard_map/ppermute | solution.py:68
  137.9 1.5 collective-permute-done.17
  139.4 10.2 %collective-permute-start.20 = (f32[36352]{0:T(1024)S(1)}, f32[36352]{0:T(1024)S(1)}, u32[]{:S(2)}, u32[]{:S(2)}) collective-permute-start(f32[36352]{0:T(1024)S(1)} %pad_maximum_fusion.2), channel_id=1, source_target_pairs={{0,1},{1,0},{2,3},{3,2},{4,5},{5,4},{6,7},{7,6},{8,9},{9,8},{10,11... | collective-permute-start | bytes 436232 | tf_op jit(solution)/shard_map/ppermute | solution.py:68
  149.6 1.4 fusion.6
  (180 shorter events, 17.2 us)
Async XLA Ops:
  0.6 8.7 %copy-start = (bf16[1,1024,128]{2,1,0:T(8,128)(2,1)S(1)}, bf16[1,1024,128]{2,1,0:T(8,128)(2,1)}, u32[]{:S(2)}) copy-start(bf16[1,1024,128]{2,1,0:T(8,128)(2,1)} %param.18) | copy-start | bytes 786436
  12.6 17.3 %copy-start.3 = (s32[1,8,96]{2,1,0:T(8,128)S(1)}, s32[1,8,96]{2,1,0:T(8,128)}, u32[]{:S(2)}) copy-start(s32[1,8,96]{2,1,0:T(8,128)} %param.22) | copy-start | bytes 9220
  12.6 17.4 %copy-start.4 = (bf16[49,128]{1,0:T(8,128)(2,1)S(1)}, bf16[49,128]{1,0:T(8,128)(2,1)}, u32[]{:S(2)}) copy-start(bf16[49,128]{1,0:T(8,128)(2,1)} %param.25) | copy-start | bytes 37636
  12.6 17.4 %copy-start.11 = (s32[1,8]{1,0:T(1,128)S(1)}, s32[1,8]{1,0:T(1,128)}, u32[]{:S(2)}) copy-start(s32[1,8]{1,0:T(1,128)} %param.21) | copy-start | bytes 100
  13.5 33.4 %all-to-all-start = ((bf16[128,9,128]{2,1,0:T(8,128)(2,1)}), bf16[128,9,128]{2,1,0:T(8,128)(2,1)S(1)}, u32[]{:S(2)}, u32[]{:S(2)}) async-start(bf16[128,9,128]{2,1,0:T(8,128)(2,1)} %pad_maximum_fusion), calls=%async_computation | async-start | bytes 1048576 | tf_op jit(solution)/shard_map/all_to_all | solution.py:205
  52.4 4.2 %collective-permute-start = (bf16[3,96,128]{2,1,0:T(8,128)(2,1)S(1)}, bf16[3,96,128]{2,1,0:T(8,128)(2,1)S(1)}, u32[]{:S(2)}, u32[]{:S(2)}) collective-permute-start(bf16[3,96,128]{2,1,0:T(8,128)(2,1)S(1)} %get-tuple-element.106), channel_id=1, source_target_pairs={{0,248},{8,0},{16,8},{24,16},{32,24},{40,32},{48,40},{56,48},{64,5... | collective-permute-start | bytes 221192 | tf_op jit(solution)/shard_map/ppermute | solution.py:15
  55.2 6.5 %collective-permute-start.1 = (bf16[3,96,128]{2,1,0:T(8,128)(2,1)S(1)}, bf16[3,96,128]{2,1,0:T(8,128)(2,1)S(1)}, u32[]{:S(2)}, u32[]{:S(2)}) collective-permute-start(bf16[3,96,128]{2,1,0:T(8,128)(2,1)S(1)} %get-tuple-element.107), channel_id=1, source_target_pairs={{0,8},{8,16},{16,24},{24,32},{32,40},{40,48},{48,56},{56,64},{64,7... | collective-permute-start | bytes 221192 | tf_op jit(solution)/shard_map/ppermute | solution.py:15
  61.7 3.4 %collective-permute-start.2 = (bf16[3,96,128]{2,1,0:T(8,128)(2,1)S(1)}, bf16[3,96,128]{2,1,0:T(8,128)(2,1)S(1)}, u32[]{:S(2)}, u32[]{:S(2)}) collective-permute-start(bf16[3,96,128]{2,1,0:T(8,128)(2,1)S(1)} %pad_maximum_fusion.4), channel_id=1, source_target_pairs={{0,6},{2,0},{4,2},{6,4},{1,7},{3,1},{5,3},{7,5},{8,14},{10,8},{12,... | collective-permute-start | bytes 221192 | tf_op jit(solution)/shard_map/ppermute | solution.py:15
  65.2 4.7 %collective-permute-start.3 = (bf16[3,96,128]{2,1,0:T(8,128)(2,1)S(1)}, bf16[3,96,128]{2,1,0:T(8,128)(2,1)S(1)}, u32[]{:S(2)}, u32[]{:S(2)}) collective-permute-start(bf16[3,96,128]{2,1,0:T(8,128)(2,1)S(1)} %pad_maximum_fusion.5), channel_id=1, source_target_pairs={{0,2},{2,4},{4,6},{6,0},{1,3},{3,5},{5,7},{7,1},{8,10},{10,12},{12... | collective-permute-start | bytes 221192 | tf_op jit(solution)/shard_map/ppermute | solution.py:15
  75.9 0.9 copy-start.7
  75.9 0.9 copy-start.8
  76.8 1.0 copy-start.1
  76.8 0.9 copy-start.9
  76.9 0.9 copy-start.10
  81.4 1.2 copy-start.12
  84.1 14.3 %collective-permute-start.4 = (f32[36352]{0:T(1024)S(1)}, f32[36352]{0:T(1024)S(1)}, u32[]{:S(2)}, u32[]{:S(2)}) collective-permute-start(f32[36352]{0:T(1024)S(1)} %slice_select_fusion), channel_id=1, source_target_pairs={{0,1},{1,0},{2,3},{3,2},{4,5},{5,4},{6,7},{7,6},{8,9},{9,8},{10,11... | collective-permute-start | bytes 436232 | tf_op jit(solution)/shard_map/ppermute | solution.py:60
  98.5 8.9 %collective-permute-start.7 = (f32[9088]{0:T(1024)S(1)}, f32[9088]{0:T(1024)S(1)}, u32[]{:S(2)}, u32[]{:S(2)}) collective-permute-start(f32[9088]{0:T(1024)S(1)} %select_select_fusion.4), channel_id=1, source_target_pairs={{0,6},{2,4},{4,2},{6,0},{1,7},{3,5},{5,3},{7,1},{8,14},{10,12},{12... | collective-permute-start | bytes 109064 | tf_op jit(solution)/shard_map/ppermute | solution.py:60
  98.8 8.6 %collective-permute-start.5 = (f32[9088]{0:T(1024)S(1)}, f32[9088]{0:T(1024)S(1)}, u32[]{:S(2)}, u32[]{:S(2)}) collective-permute-start(f32[9088]{0:T(1024)S(1)} %get-tuple-element.117), channel_id=1, source_target_pairs={{0,2},{2,0},{4,6},{6,4},{1,3},{3,1},{5,7},{7,5},{8,10},{10,8},{12,... | collective-permute-start | bytes 109064 | tf_op jit(solution)/shard_map/ppermute | solution.py:60
  98.9 8.5 %collective-permute-start.6 = (f32[9088]{0:T(1024)S(1)}, f32[9088]{0:T(1024)S(1)}, u32[]{:S(2)}, u32[]{:S(2)}) collective-permute-start(f32[9088]{0:T(1024)S(1)} %get-tuple-element.118), channel_id=1, source_target_pairs={{0,4},{2,6},{4,0},{6,2},{1,5},{3,7},{5,1},{7,3},{8,12},{10,14},{12... | collective-permute-start | bytes 109064 | tf_op jit(solution)/shard_map/ppermute | solution.py:60
  102.5 8.1 %collective-permute-start.9 = (bf16[3,96,128]{2,1,0:T(8,128)(2,1)S(1)}, bf16[3,96,128]{2,1,0:T(8,128)(2,1)S(1)}, u32[]{:S(2)}, u32[]{:S(2)}) collective-permute-start(bf16[3,96,128]{2,1,0:T(8,128)(2,1)S(1)} %get-tuple-element.102), channel_id=1, source_target_pairs={{0,8},{8,16},{16,24},{24,32},{32,40},{40,48},{48,56},{56,64},{64,7... | collective-permute-start | bytes 221192 | tf_op jit(solution)/shard_map/ppermute | solution.py:15
  102.6 8.0 %collective-permute-start.10 = (bf16[3,96,128]{2,1,0:T(8,128)(2,1)S(1)}, bf16[3,96,128]{2,1,0:T(8,128)(2,1)S(1)}, u32[]{:S(2)}, u32[]{:S(2)}) collective-permute-start(bf16[3,96,128]{2,1,0:T(8,128)(2,1)S(1)} %get-tuple-element.103), channel_id=1, source_target_pairs={{0,248},{8,0},{16,8},{24,16},{32,24},{40,32},{48,40},{56,48},{64,5... | collective-permute-start | bytes 221192 | tf_op jit(solution)/shard_map/ppermute | solution.py:15
  107.5 3.2 %collective-permute-start.8 = (f32[9088]{0:T(1024)S(1)}, f32[9088]{0:T(1024)S(1)}, u32[]{:S(2)}, u32[]{:S(2)}) collective-permute-start(f32[9088]{0:T(1024)S(1)} %add_add_fusion), channel_id=1, source_target_pairs={{0,8},{8,0},{16,24},{24,16},{32,40},{40,32},{48,56},{56,48},{64,72... | collective-permute-start | bytes 109064 | tf_op jit(solution)/shard_map/ppermute | solution.py:63
  110.7 4.5 %collective-permute-start.13 = (bf16[3,96,128]{2,1,0:T(8,128)(2,1)S(1)}, bf16[3,96,128]{2,1,0:T(8,128)(2,1)S(1)}, u32[]{:S(2)}, u32[]{:S(2)}) collective-permute-start(bf16[3,96,128]{2,1,0:T(8,128)(2,1)S(1)} %pad_maximum_fusion.6), channel_id=1, source_target_pairs={{0,2},{2,4},{4,6},{6,0},{1,3},{3,5},{5,7},{7,1},{8,10},{10,12},{12... | collective-permute-start | bytes 221192 | tf_op jit(solution)/shard_map/ppermute | solution.py:15
  115.3 10.6 %collective-permute-start.14 = (bf16[3,96,128]{2,1,0:T(8,128)(2,1)S(1)}, bf16[3,96,128]{2,1,0:T(8,128)(2,1)S(1)}, u32[]{:S(2)}, u32[]{:S(2)}) collective-permute-start(bf16[3,96,128]{2,1,0:T(8,128)(2,1)S(1)} %pad_maximum_fusion.7), channel_id=1, source_target_pairs={{0,6},{2,0},{4,2},{6,4},{1,7},{3,1},{5,3},{7,5},{8,14},{10,8},{12,... | collective-permute-start | bytes 221192 | tf_op jit(solution)/shard_map/ppermute | solution.py:15
  115.4 3.8 %collective-permute-start.11 = (f32[9088]{0:T(1024)S(1)}, f32[9088]{0:T(1024)S(1)}, u32[]{:S(2)}, u32[]{:S(2)}) collective-permute-start(f32[9088]{0:T(1024)S(1)} %add.608), channel_id=1, source_target_pairs={{0,16},{8,24},{16,0},{24,8},{32,48},{40,56},{48,32},{56,40},{64,80... | collective-permute-start | bytes 109064 | tf_op jit(solution)/shard_map/ppermute | solution.py:63
  119.2 6.7 %collective-permute-start.12 = (f32[9088]{0:T(1024)S(1)}, f32[9088]{0:T(1024)S(1)}, u32[]{:S(2)}, u32[]{:S(2)}) collective-permute-start(f32[9088]{0:T(1024)S(1)} %add.609), channel_id=1, source_target_pairs={{0,32},{8,40},{16,48},{24,56},{32,0},{40,8},{48,16},{56,24},{64,96... | collective-permute-start | bytes 109064 | tf_op jit(solution)/shard_map/ppermute | solution.py:63
  126.0 2.9 %collective-permute-start.15 = (f32[9088]{0:T(1024)S(1)}, f32[9088]{0:T(1024)S(1)}, u32[]{:S(2)}, u32[]{:S(2)}) collective-permute-start(f32[9088]{0:T(1024)S(1)} %add.610), channel_id=1, source_target_pairs={{0,64},{8,72},{16,80},{24,88},{32,96},{40,104},{48,112},{56,120},{... | collective-permute-start | bytes 109064 | tf_op jit(solution)/shard_map/ppermute | solution.py:63
  128.9 4.3 %collective-permute-start.16 = (f32[9088]{0:T(1024)S(1)}, f32[9088]{0:T(1024)S(1)}, u32[]{:S(2)}, u32[]{:S(2)}) collective-permute-start(f32[9088]{0:T(1024)S(1)} %add.612), channel_id=1, source_target_pairs={{0,128},{8,136},{16,144},{24,152},{32,160},{40,168},{48,176},{56,1... | collective-permute-start | bytes 109064 | tf_op jit(solution)/shard_map/ppermute | solution.py:63
  133.2 4.0 %collective-permute-start.19 = (f32[9088]{0:T(1024)S(1)}, f32[9088]{0:T(1024)S(1)}, u32[]{:S(2)}, u32[]{:S(2)}) collective-permute-start(f32[9088]{0:T(1024)S(1)} %add.613), channel_id=1, source_target_pairs={{0,6},{2,4},{4,2},{6,0},{1,7},{3,5},{5,3},{7,1},{8,14},{10,12},{12... | collective-permute-start | bytes 109064 | tf_op jit(solution)/shard_map/ppermute | solution.py:68
  133.2 4.7 %collective-permute-start.18 = (f32[9088]{0:T(1024)S(1)}, f32[9088]{0:T(1024)S(1)}, u32[]{:S(2)}, u32[]{:S(2)}) collective-permute-start(f32[9088]{0:T(1024)S(1)} %add.613), channel_id=1, source_target_pairs={{0,4},{2,6},{4,0},{6,2},{1,5},{3,7},{5,1},{7,3},{8,12},{10,14},{12... | collective-permute-start | bytes 109064 | tf_op jit(solution)/shard_map/ppermute | solution.py:68
  136.6 2.8 %collective-permute-start.17 = (f32[9088]{0:T(1024)S(1)}, f32[9088]{0:T(1024)S(1)}, u32[]{:S(2)}, u32[]{:S(2)}) collective-permute-start(f32[9088]{0:T(1024)S(1)} %add.613), channel_id=1, source_target_pairs={{0,2},{2,0},{4,6},{6,4},{1,3},{3,1},{5,7},{7,5},{8,10},{10,8},{12,... | collective-permute-start | bytes 109064 | tf_op jit(solution)/shard_map/ppermute | solution.py:68
  139.4 11.6 %collective-permute-start.20 = (f32[36352]{0:T(1024)S(1)}, f32[36352]{0:T(1024)S(1)}, u32[]{:S(2)}, u32[]{:S(2)}) collective-permute-start(f32[36352]{0:T(1024)S(1)} %pad_maximum_fusion.2), channel_id=1, source_target_pairs={{0,1},{1,0},{2,3},{3,2},{4,5},{5,4},{6,7},{7,6},{8,9},{9,8},{10,11... | collective-permute-start | bytes 436232 | tf_op jit(solution)/shard_map/ppermute | solution.py:68
  (3 other events, 2.5 us)
